TPU v7x, 128 devices: a whole 4x4x4 slice. The times are simulated.
128 devices in a mesh: node: 4 (over z), local: 32 (over x, y, core).
Axes of the slice: x: 4, y: 4, z: 4, core: 2. Of those that a mesh axis runs over, the one named last changes fastest.
Arguments:
- tokens: bfloat16 [16384, 3584], P(('node', 'local')), may hold values from -6 to 6
- group_ids: int32 [16384, 2], P(('node', 'local')), may hold values from 0 to 3, as said below
- local_ids: int32 [16384, 8], P(('node', 'local')), may hold values from 0 to 31, as said below
- router: bfloat16 [3584, 128], replicated, may hold values from -0.09375 to 0.09375
- w_gate: bfloat16 [128, 3584, 1024], P(('node', 'local')), may hold values from -0.09375 to 0.09375
- w_up: bfloat16 [128, 3584, 1024], P(('node', 'local')), may hold values from -0.09375 to 0.09375
- w_down: bfloat16 [128, 1024, 3584], P(('node', 'local')), may hold values from -0.1875 to 0.1875
Outputs:
- moe_out: bfloat16 [16384, 3584], P(('node', 'local'))
Inputs may be any that keep to these rules, and one draw needn't show every extreme that they name: `group_ids`: each token names two different node groups; the tokens of one device name every node group exactly 64 times. `local_ids`: entry k names an expert of node group group_ids[t, k // 4]; the four entries of one group are different. The tokens of one device route at most 10 tokens to one expert, and in every node group some expert receives exactly 10 tokens from every device.
All inputs are finite; a program needn't handle non-finite values.
Results may differ from a plain program's by a relative error of at most 0.0058.
Values may be sent and summed in bfloat16 or wider, within the bound.
No kernel may reach another device: no remote copies, remote signals or barrier semaphores. Data moves between devices by JAX's collectives and lax.ppermute only.
A program may use at most 128 MiB of HBM per device.

v0:
```python
import jax
import jax.numpy as jnp
from jax import lax
from jax.sharding import PartitionSpec as P

LANES = 128


def slot_positions(targets, bins):
    onehot = (targets[:, None] == jnp.arange(bins, dtype=jnp.int32)[None, :]).astype(jnp.int32)
    earlier = jnp.cumsum(onehot, axis=0) - onehot
    return jnp.sum(earlier * onehot, axis=1)


def slot_pieces(cap_rows, feat_width):
    tile_rows = 8 * LANES // feat_width if feat_width < 8 * LANES else 1
    whole = [p for p in range(1, cap_rows) if (p * feat_width // LANES) % 8 == 0 and ((cap_rows - p) * feat_width // LANES) % 8 == 0]
    if not whole or cap_rows * feat_width % LANES:
        return (cap_rows,)
    first = min(whole, key=lambda p: abs(2 * p - cap_rows) + (p < cap_rows - p))
    return (first, cap_rows - first)


def combine_piece(rows, weights, flat_ids, positions, start, size):
    tok_dev, picks = weights.shape
    inside = ((positions >= start) & (positions < start + size)).reshape(tok_dev, picks)
    slot = (flat_ids * size + positions - start).reshape(tok_dev, picks)
    hits = slot[:, :, None] == jnp.arange(rows.shape[0], dtype=jnp.int32)[None, None, :]
    dense = jnp.sum(jnp.where(hits & inside[:, :, None], weights[:, :, None], 0.0), axis=1)
    high = dense.astype(jnp.bfloat16)
    low = (dense - high.astype(jnp.float32)).astype(jnp.bfloat16)
    return jnp.dot(high, rows, preferred_element_type=jnp.float32) + jnp.dot(
        low, rows, preferred_element_type=jnp.float32
    )


def expert_rows(flat_rows, w_gate, w_up, w_down):
    gate_part = jnp.dot(flat_rows, w_gate[0], preferred_element_type=jnp.float32)
    up_part = jnp.dot(flat_rows, w_up[0], preferred_element_type=jnp.float32)
    hidden = (jax.nn.silu(gate_part) * up_part).astype(jnp.bfloat16)
    return jnp.dot(hidden, w_down[0], preferred_element_type=jnp.float32).astype(jnp.bfloat16)


def on_device(tokens, group_ids, local_ids, router, w_gate, w_up, w_down):
    tok_dev, feat_width = tokens.shape
    node_size = lax.axis_size("node")
    local_size = lax.axis_size("local")
    experts_all = node_size * local_size
    cap_rows = 5 * tok_dev // (2 * local_size)
    group_count = group_ids.shape[1]
    per_group = local_ids.shape[1] // group_count
    expert_ids = jnp.repeat(group_ids, per_group, axis=1) * local_size + local_ids
    affinity = jax.nn.sigmoid(jnp.dot(tokens, router, preferred_element_type=jnp.float32))
    picked = jnp.take_along_axis(affinity, expert_ids, axis=1)
    picked_total = jnp.sum(picked, axis=1)
    flat_ids = expert_ids.reshape(-1)
    positions = slot_positions(flat_ids, experts_all)
    owners = jnp.arange(flat_ids.shape[0], dtype=jnp.int32) // local_ids.shape[1]
    src_table = jnp.full((experts_all, cap_rows), tok_dev, jnp.int32).at[flat_ids, positions].set(owners)
    padded = jnp.concatenate([tokens, jnp.zeros((1, feat_width), tokens.dtype)], axis=0)
    pieces = slot_pieces(cap_rows, feat_width)
    weights = 2.5 * picked / picked_total[:, None]
    mixed = jnp.zeros((tok_dev, feat_width), jnp.float32)
    start = 0
    for size in pieces:
        wire = (experts_all, size * feat_width // LANES, LANES)
        send_rows = padded[src_table[:, start:start + size].reshape(-1)].reshape(wire)
        received = lax.all_to_all(send_rows, ("node", "local"), split_axis=0, concat_axis=0, tiled=True)
        produced = expert_rows(received.reshape(-1, feat_width), w_gate, w_up, w_down).reshape(wire)
        returned = lax.all_to_all(produced, ("node", "local"), split_axis=0, concat_axis=0, tiled=True)
        mixed = mixed + combine_piece(returned.reshape(-1, feat_width), weights, flat_ids, positions, start, size)
        start += size
    return mixed.astype(jnp.bfloat16)


def solution(mesh):
    return jax.shard_map(
        on_device,
        mesh=mesh,
        in_specs=(
            P(("node", "local"), None),
            P(("node", "local"), None),
            P(("node", "local"), None),
            P(),
            P(("node", "local"), None, None),
            P(("node", "local"), None, None),
            P(("node", "local"), None, None),
        ),
        out_specs=P(("node", "local"), None),
        check_vma=False,
    )
```

profile of v0, /device:TPU:14, one launch (start us, length us, event | category | flops | bytes accessed | tf_op | source)
XLA Modules:
  0.0 304.1 jit_solution(16762994126757251560)
XLA Ops:
  0.0 0.8 broadcast_multiply_fusion
  3.0 0.7 and_reduce_fusion
  4.5 4.3 %scatter_custom_fusion = s32[1280]{0:T(1024)S(1)} fusion(s32[1024]{0:T(1024)S(1)} %broadcast_select_fusion, s32[1024]{0:T(1024)S(1)} %add_select_fusion, s32[]{:T(128)} %constant.32.clone.1), kind=kCustom, calls=%fused_computation.70 | custom fusion | bytes 5124
  9.2 4.2 %gather_fusion.1 = bf16[512,3584]{1,0:T(8,128)(2,1)} fusion(bf16[129,3584]{1,0:T(8,128)(2,1)S(1)} %concatenate.6, s32[1024]{0:T(1024)S(1)} %pad_clamp_fusion), kind=kCustom, calls=%fused_computation.1 | custom fusion | bytes 7342080 | tf_op jit(solution)/shard_map/gather | solution.py:67
  13.3 8.0 %reshape.213 = bf16[128,112,128]{2,1,0:T(8,128)(2,1)} reshape(bf16[512,3584]{1,0:T(8,128)(2,1)} %gather_fusion.1) | data formatting | bytes 7340032 | tf_op jit(solution)/shard_map/reshape | solution.py:67
  21.3 10.8 %all-to-all-start.2 = ((bf16[128,112,128]{2,1,0:T(8,128)(2,1)}), bf16[128,112,128]{2,1,0:T(8,128)(2,1)}, u32[]{:S(2)}, u32[]{:S(2)}) async-start(bf16[128,112,128]{2,1,0:T(8,128)(2,1)} %reshape.213), calls=%async_computation.2 | async-start | bytes 7340032 | tf_op jit(solution)/shard_map/all_to_all | solution.py:68
  32.4 5.4 %gather_fusion = bf16[768,3584]{1,0:T(8,128)(2,1)} fusion(bf16[129,3584]{1,0:T(8,128)(2,1)S(1)} %concatenate.6, s32[1024]{0:T(1024)S(1)} %pad_clamp_fusion.1), kind=kCustom, calls=%fused_computation | custom fusion | bytes 11013120 | tf_op jit(solution)/shard_map/gather | solution.py:67
  37.8 11.2 %reshape.208 = bf16[128,168,128]{2,1,0:T(8,128)(2,1)} reshape(bf16[768,3584]{1,0:T(8,128)(2,1)} %gather_fusion) | data formatting | bytes 11010048 | tf_op jit(solution)/shard_map/reshape | solution.py:67
  49.0 27.7 %all-to-all-done.2 = bf16[128,112,128]{2,1,0:T(8,128)(2,1)} async-done(((bf16[128,112,128]{2,1,0:T(8,128)(2,1)}), bf16[128,112,128]{2,1,0:T(8,128)(2,1)}, u32[]{:S(2)}, u32[]{:S(2)}) %all-to-all-start.2) | async-done | bytes 3670048 | tf_op jit(solution)/shard_map/all_to_all | solution.py:68
  76.6 8.2 %all-to-all-start = ((bf16[128,168,128]{2,1,0:T(8,128)(2,1)}), bf16[128,168,128]{2,1,0:T(8,128)(2,1)}, u32[]{:S(2)}, u32[]{:S(2)}) async-start(bf16[128,168,128]{2,1,0:T(8,128)(2,1)} %reshape.208), calls=%async_computation | async-start | bytes 11010048 | tf_op jit(solution)/shard_map/all_to_all | solution.py:68
  84.8 7.7 %reshape.214 = bf16[512,3584]{1,0:T(8,128)(2,1)} reshape(bf16[128,112,128]{2,1,0:T(8,128)(2,1)} %all-to-all-done.2) | data formatting | bytes 7340032 | tf_op jit(solution)/shard_map/reshape | solution.py:69
  92.5 9.5 %fusion.4 = f32[512,1024]{1,0:T(8,128)} fusion(bf16[512,3584]{1,0:T(8,128)(2,1)} %reshape.214, bf16[1,3584,1024]{2,1,0:T(8,128)(2,1)} %param.12), kind=kOutput, calls=%fused_computation.8 | convolution fusion | flops 3758096384 | bytes 13107200 | tf_op jit(solution)/shard_map/dot_general | solution.py:39
  101.9 16.7 %fusion.15 = bf16[512,3584]{1,0:T(8,128)(2,1)} fusion(bf16[1,1024,3584]{2,1,0:T(8,128)(2,1)} %param.13, f32[512,1024]{1,0:T(8,128)} %fusion.4, bf16[512,3584]{1,0:T(8,128)(2,1)} %reshape.214, bf16[1,3584,1024]{2,1,0:T(8,128)(2,1)} %param.11), kind=kOutput, calls=%fused_computation.17 | convolution fusion | flops 7521173504 | bytes 24117248 | tf_op jit(solution)/shard_map/dot_general | solution.py:41
  118.6 8.0 %reshape.215 = bf16[128,112,128]{2,1,0:T(8,128)(2,1)} reshape(bf16[512,3584]{1,0:T(8,128)(2,1)} %fusion.15) | data formatting | bytes 7340032 | tf_op jit(solution)/shard_map/reshape | solution.py:69
  126.6 23.7 %all-to-all-done = bf16[128,168,128]{2,1,0:T(8,128)(2,1)} async-done(((bf16[128,168,128]{2,1,0:T(8,128)(2,1)}), bf16[128,168,128]{2,1,0:T(8,128)(2,1)}, u32[]{:S(2)}, u32[]{:S(2)}) %all-to-all-start) | async-done | bytes 5505056 | tf_op jit(solution)/shard_map/all_to_all | solution.py:68
  150.3 6.9 %all-to-all-start.3 = ((bf16[128,112,128]{2,1,0:T(8,128)(2,1)}), bf16[128,112,128]{2,1,0:T(8,128)(2,1)}, u32[]{:S(2)}, u32[]{:S(2)}) async-start(bf16[128,112,128]{2,1,0:T(8,128)(2,1)} %reshape.215), calls=%async_computation.3 | async-start | bytes 7340032 | tf_op jit(solution)/shard_map/all_to_all | solution.py:70
  157.2 10.7 %reshape.209 = bf16[768,3584]{1,0:T(8,128)(2,1)} reshape(bf16[128,168,128]{2,1,0:T(8,128)(2,1)} %all-to-all-done) | data formatting | bytes 11010048 | tf_op jit(solution)/shard_map/reshape | solution.py:69
  167.8 10.9 %fusion.6 = f32[768,1024]{1,0:T(8,128)} fusion(bf16[768,3584]{1,0:T(8,128)(2,1)} %reshape.209, bf16[1,3584,1024]{2,1,0:T(8,128)(2,1)} %param.12), kind=kOutput, calls=%fused_computation.10 | convolution fusion | flops 5637144576 | bytes 15990784 | tf_op jit(solution)/shard_map/dot_general | solution.py:39
  178.7 20.0 %fusion.12 = bf16[768,3584]{1,0:T(8,128)(2,1)} fusion(bf16[1,1024,3584]{2,1,0:T(8,128)(2,1)} %param.13, f32[768,1024]{1,0:T(8,128)} %fusion.6, bf16[768,3584]{1,0:T(8,128)(2,1)} %reshape.209, bf16[1,3584,1024]{2,1,0:T(8,128)(2,1)} %param.11), kind=kOutput, calls=%fused_computation.16 | convolution fusion | flops 11281760256 | bytes 28835840 | tf_op jit(solution)/shard_map/dot_general | solution.py:41
  198.7 11.1 %reshape.210 = bf16[128,168,128]{2,1,0:T(8,128)(2,1)} reshape(bf16[768,3584]{1,0:T(8,128)(2,1)} %fusion.12) | data formatting | bytes 11010048 | tf_op jit(solution)/shard_map/reshape | solution.py:69
  209.8 10.2 %all-to-all-start.1 = ((bf16[128,168,128]{2,1,0:T(8,128)(2,1)}), bf16[128,168,128]{2,1,0:T(8,128)(2,1)}, u32[]{:S(2)}, u32[]{:S(2)}) async-start(bf16[128,168,128]{2,1,0:T(8,128)(2,1)} %reshape.210), calls=%async_computation.1 | async-start | bytes 11010048 | tf_op jit(solution)/shard_map/all_to_all | solution.py:70
  220.8 6.8 %gather_fusion.2 = f32[1024]{0:T(1024)S(1)} fusion(f32[128,128]{1,0:T(8,128)S(1)} %fusion.31, s32[1024]{0:T(1024)S(1)} %reshape.237), kind=kCustom, calls=%fused_computation.2 | custom fusion | bytes 16384 | tf_op jit(solution)/shard_map/jit(take_along_axis)/gather | solution.py:54
  228.4 1.0 select_reduce_fusion.1
  229.4 1.4 select_reduce_fusion
  230.9 7.7 %reshape.216 = bf16[512,3584]{1,0:T(8,128)(2,1)} reshape(bf16[128,112,128]{2,1,0:T(8,128)(2,1)} %all-to-all-done.3) | data formatting | bytes 7340032 | tf_op jit(solution)/shard_map/reshape | solution.py:71
  238.5 2.7 fusion.43
  241.2 44.3 %all-to-all-done.1 = bf16[128,168,128]{2,1,0:T(8,128)(2,1)} async-done(((bf16[128,168,128]{2,1,0:T(8,128)(2,1)}), bf16[128,168,128]{2,1,0:T(8,128)(2,1)}, u32[]{:S(2)}, u32[]{:S(2)}) %all-to-all-start.1) | async-done | bytes 5505056 | tf_op jit(solution)/shard_map/all_to_all | solution.py:70
  285.5 10.6 %reshape.211 = bf16[768,3584]{1,0:T(8,128)(2,1)} reshape(bf16[128,168,128]{2,1,0:T(8,128)(2,1)} %all-to-all-done.1) | data formatting | bytes 11010048 | tf_op jit(solution)/shard_map/reshape | solution.py:71
  296.2 3.6 %fusion.40 = f32[128,3584]{1,0:T(8,128)S(1)} fusion(bf16[768,3584]{1,0:T(8,128)(2,1)} %reshape.211, f32[128,768]{1,0:T(8,128)S(1)} %select_reduce_fusion), kind=kOutput, calls=%fused_computation.47 | convolution fusion | flops 704741376 | bytes 7733248 | tf_op jit(solution)/shard_map/dot_general | solution.py:32
  300.3 0.9 convolution_add_fusion.1
  301.3 1.1 copy-done.2
  302.4 1.7 fusion.19
  (57 shorter events, 5.5 us)
Async XLA Ops:
  0.0 220.3 %copy-start = (bf16[3584,128]{1,0:T(8,128)(2,1)S(1)}, bf16[3584,128]{1,0:T(8,128)(2,1)}, u32[]{:S(2)}) copy-start(bf16[3584,128]{1,0:T(8,128)(2,1)} %param.10) | copy-start | bytes 2752516
  0.0 9.1 %copy-start.3 = (bf16[128,3584]{1,0:T(8,128)(2,1)S(1)}, bf16[128,3584]{1,0:T(8,128)(2,1)}, u32[]{:S(2)}) copy-start(bf16[128,3584]{1,0:T(8,128)(2,1)} %param.7) | copy-start | bytes 2752516
  1.5 0.6 copy-start.4
  21.3 55.3 %all-to-all-start.2 = ((bf16[128,112,128]{2,1,0:T(8,128)(2,1)}), bf16[128,112,128]{2,1,0:T(8,128)(2,1)}, u32[]{:S(2)}, u32[]{:S(2)}) async-start(bf16[128,112,128]{2,1,0:T(8,128)(2,1)} %reshape.213), calls=%async_computation.2 | async-start | bytes 7340032 | tf_op jit(solution)/shard_map/all_to_all | solution.py:68
  76.6 73.7 %all-to-all-start = ((bf16[128,168,128]{2,1,0:T(8,128)(2,1)}), bf16[128,168,128]{2,1,0:T(8,128)(2,1)}, u32[]{:S(2)}, u32[]{:S(2)}) async-start(bf16[128,168,128]{2,1,0:T(8,128)(2,1)} %reshape.208), calls=%async_computation | async-start | bytes 11010048 | tf_op jit(solution)/shard_map/all_to_all | solution.py:68
  150.3 59.6 %all-to-all-start.3 = ((bf16[128,112,128]{2,1,0:T(8,128)(2,1)}), bf16[128,112,128]{2,1,0:T(8,128)(2,1)}, u32[]{:S(2)}, u32[]{:S(2)}) async-start(bf16[128,112,128]{2,1,0:T(8,128)(2,1)} %reshape.215), calls=%async_computation.3 | async-start | bytes 7340032 | tf_op jit(solution)/shard_map/all_to_all | solution.py:70
  209.8 75.7 %all-to-all-start.1 = ((bf16[128,168,128]{2,1,0:T(8,128)(2,1)}), bf16[128,168,128]{2,1,0:T(8,128)(2,1)}, u32[]{:S(2)}, u32[]{:S(2)}) async-start(bf16[128,168,128]{2,1,0:T(8,128)(2,1)} %reshape.210), calls=%async_computation.1 | async-start | bytes 11010048 | tf_op jit(solution)/shard_map/all_to_all | solution.py:70
  220.8 7.0 %copy-start.5 = (s32[128,8]{0,1:T(8,128)S(1)}, s32[128,8]{0,1:T(8,128)}, u32[]{:S(2)}) copy-start(s32[128,8]{0,1:T(8,128)} %copy-done.4) | copy-start | bytes 12292
  296.2 4.2 %copy-start.1 = (bf16[768,3584]{1,0:T(8,128)(2,1)S(1)}, bf16[768,3584]{1,0:T(8,128)(2,1)}, u32[]{:S(2)}) copy-start(bf16[768,3584]{1,0:T(8,128)(2,1)} %reshape.211) | copy-start | bytes 16515076
  300.3 2.0 copy-start.2
where the time goes:
time: 309 us; the launch traced here: 304 us
  local copies, waits for them, and re-layouts  99.7 us (32%)
  waiting for transfers between devices  95.6 us (31%)
  matrix products  66.3 us (21%)
  starting transfers between devices  36 us (12%)
  other arithmetic  6.16 us (2%)
    all_to_all x2, waiting for transfers between devices, on_device(): lax.all_to_all(send_rows, ('node', 'local'), split_axis=0, concat_axis=0,...  51.3 us
    all_to_all x2, waiting for transfers between devices, on_device(): lax.all_to_all(produced, ('node', 'local'), split_axis=0, concat_axis=0,...  44.3 us
    dot_general x2, matrix products, expert_rows(): jnp.dot(hidden, w_down[0], preferred_element_type=jnp.float32)  36.6 us
    dot_general x2, matrix products, expert_rows(): up_part = jnp.dot(flat_rows, w_up[0], preferred_element_type=jnp.float32)  20.4 us
    reshape x2, local copies, waits for them, and re-layouts, on_device(): padded[src_table[:, start:start + size].reshape(-1)].reshape(wire)  19.1 us
    reshape x2, local copies, waits for them, and re-layouts, on_device(): expert_rows(received.reshape(-1, feat_width), w_gate, w_up, w_down)  19.1 us
    all_to_all x2, starting transfers between devices, on_device(): lax.all_to_all(send_rows, ('node', 'local'), split_axis=0, concat_axis=0,...  18.9 us
    reshape x2, local copies, waits for them, and re-layouts, on_device(): received.reshape(-1, feat_width)  18.4 us
  transfers between devices with their start and end apart: 4, of which 3 were waited for; matrix products, arithmetic and copies ran while one was open for 44% of the time, Pallas kernels for 0%

commit v1 on v0

--- a/solution.py
+++ b/solution.py
@@ -21,14 +21,24 @@
     return (first, cap_rows - first)
 
 
+def gather_piece(tokens, flat_ids, positions, start, size, experts_all):
+    tok_dev = tokens.shape[0]
+    inside = (positions >= start) & (positions < start + size)
+    slot = jnp.where(inside, flat_ids * size + positions - start, -1).reshape(tok_dev, -1)
+    hits = slot[None, :, :] == jnp.arange(experts_all * size, dtype=jnp.int32)[:, None, None]
+    onehot = jnp.any(hits, axis=2).astype(tokens.dtype)
+    return jnp.dot(onehot, tokens, preferred_element_type=jnp.float32).astype(tokens.dtype)
+
+
 def combine_piece(rows, weights, flat_ids, positions, start, size):
     tok_dev, picks = weights.shape
     inside = ((positions >= start) & (positions < start + size)).reshape(tok_dev, picks)
     slot = (flat_ids * size + positions - start).reshape(tok_dev, picks)
     hits = slot[:, :, None] == jnp.arange(rows.shape[0], dtype=jnp.int32)[None, None, :]
     dense = jnp.sum(jnp.where(hits & inside[:, :, None], weights[:, :, None], 0.0), axis=1)
-    high = dense.astype(jnp.bfloat16)
-    low = (dense - high.astype(jnp.float32)).astype(jnp.bfloat16)
+    high_part = lax.reduce_precision(dense, exponent_bits=8, mantissa_bits=7)
+    high = high_part.astype(jnp.bfloat16)
+    low = (dense - high_part).astype(jnp.bfloat16)
     return jnp.dot(high, rows, preferred_element_type=jnp.float32) + jnp.dot(
         low, rows, preferred_element_type=jnp.float32
     )
@@ -55,16 +65,13 @@
     picked_total = jnp.sum(picked, axis=1)
     flat_ids = expert_ids.reshape(-1)
     positions = slot_positions(flat_ids, experts_all)
-    owners = jnp.arange(flat_ids.shape[0], dtype=jnp.int32) // local_ids.shape[1]
-    src_table = jnp.full((experts_all, cap_rows), tok_dev, jnp.int32).at[flat_ids, positions].set(owners)
-    padded = jnp.concatenate([tokens, jnp.zeros((1, feat_width), tokens.dtype)], axis=0)
     pieces = slot_pieces(cap_rows, feat_width)
     weights = 2.5 * picked / picked_total[:, None]
     mixed = jnp.zeros((tok_dev, feat_width), jnp.float32)
     start = 0
     for size in pieces:
         wire = (experts_all, size * feat_width // LANES, LANES)
-        send_rows = padded[src_table[:, start:start + size].reshape(-1)].reshape(wire)
+        send_rows = gather_piece(tokens, flat_ids, positions, start, size, experts_all).reshape(wire)
         received = lax.all_to_all(send_rows, ("node", "local"), split_axis=0, concat_axis=0, tiled=True)
         produced = expert_rows(received.reshape(-1, feat_width), w_gate, w_up, w_down).reshape(wire)
         returned = lax.all_to_all(produced, ("node", "local"), split_axis=0, concat_axis=0, tiled=True)

time: 309 us -> 302 us (0.977)
  local copies, waits for them, and re-layouts: 99.7 us -> 84.9 us
  matrix products: 66.3 us -> 73.2 us
    gather x2 -> x0, local copies, waits for them, and re-layouts: 9.58 us -> none  [on_device(): padded[src_table[:, start:start + size].reshape(-1)].reshape(wire)]
    dot_general x0 -> x2, matrix products: none -> 6.85 us  [gather_piece(): jnp.dot(onehot, tokens, preferred_element_type=jnp.float32)]
    unnamed x13 -> x8, local copies, waits for them, and re-layouts: 6.23 us -> 1.7 us
    reshape x5 -> x2, local copies, waits for them, and re-layouts: 19.5 us -> 19.1 us  [on_device(): gather_piece(tokens, flat_ids, positions, start, size, experts_all)]
where the time goes in v1:
time: 302 us; the launch traced here: 297 us
  waiting for transfers between devices  96.2 us (32%)
  local copies, waits for them, and re-layouts  84.9 us (28%)
  matrix products  73.2 us (24%)
  starting transfers between devices  36 us (12%)
  other arithmetic  6.86 us (2%)
    all_to_all x2, waiting for transfers between devices, on_device(): lax.all_to_all(send_rows, ('node', 'local'), split_axis=0, concat_axis=0,...  51.7 us
    all_to_all x2, waiting for transfers between devices, on_device(): lax.all_to_all(produced, ('node', 'local'), split_axis=0, concat_axis=0,...  44.5 us
    dot_general x2, matrix products, expert_rows(): jnp.dot(hidden, w_down[0], preferred_element_type=jnp.float32)  36.7 us
    dot_general x2, matrix products, expert_rows(): up_part = jnp.dot(flat_rows, w_up[0], preferred_element_type=jnp.float32)  20.4 us
    reshape x2, local copies, waits for them, and re-layouts, on_device(): gather_piece(tokens, flat_ids, positions, start, size, experts_all)  19.1 us
    reshape x2, local copies, waits for them, and re-layouts, on_device(): expert_rows(received.reshape(-1, feat_width), w_gate, w_up, w_down)  19.1 us
    all_to_all x2, starting transfers between devices, on_device(): lax.all_to_all(send_rows, ('node', 'local'), split_axis=0, concat_axis=0,...  18.9 us
    reshape x2, local copies, waits for them, and re-layouts, on_device(): received.reshape(-1, feat_width)  18.4 us
  transfers between devices with their start and end apart: 4, of which 3 were waited for; matrix products, arithmetic and copies ran while one was open for 44% of the time, Pallas kernels for 0%

profile of v1, /device:TPU:14, one launch (start us, length us, event | category | flops | bytes accessed | tf_op | source)
XLA Modules:
  0.0 297.3 jit_solution(17884378845526671545)
XLA Ops:
  0.0 0.8 broadcast_multiply_fusion
  2.8 0.9 fusion.27
  3.7 2.9 convolution_convert_fusion.1
  6.6 8.0 %reshape.130 = bf16[128,112,128]{2,1,0:T(8,128)(2,1)} reshape(bf16[512,3584]{1,0:T(8,128)(2,1)} %convolution_convert_fusion.1) | data formatting | bytes 7340032 | tf_op jit(solution)/shard_map/reshape | solution.py:74
  14.6 10.8 %all-to-all-start.2 = ((bf16[128,112,128]{2,1,0:T(8,128)(2,1)}), bf16[128,112,128]{2,1,0:T(8,128)(2,1)}, u32[]{:S(2)}, u32[]{:S(2)}) async-start(bf16[128,112,128]{2,1,0:T(8,128)(2,1)} %reshape.130), calls=%async_computation.2 | async-start | bytes 7340032 | tf_op jit(solution)/shard_map/all_to_all | solution.py:75
  25.3 1.4 fusion.21
  26.7 4.0 %convolution_convert_fusion = bf16[768,3584]{1,0:T(8,128)(2,1)} fusion(pred[768,128]{1,0:T(8,128)(4,1)S(1)} %fusion.21, bf16[128,3584]{1,0:T(8,128)(2,1)S(1)} %copy-done), kind=kOutput, calls=%fused_computation.13 | convolution fusion | flops 707395584 | bytes 6520832 | tf_op jit(solution)/shard_map/dot_general | solution.py:30
  30.7 11.2 %reshape.126 = bf16[128,168,128]{2,1,0:T(8,128)(2,1)} reshape(bf16[768,3584]{1,0:T(8,128)(2,1)} %convolution_convert_fusion) | data formatting | bytes 11010048 | tf_op jit(solution)/shard_map/reshape | solution.py:74
  41.9 28.0 %all-to-all-done.2 = bf16[128,112,128]{2,1,0:T(8,128)(2,1)} async-done(((bf16[128,112,128]{2,1,0:T(8,128)(2,1)}), bf16[128,112,128]{2,1,0:T(8,128)(2,1)}, u32[]{:S(2)}, u32[]{:S(2)}) %all-to-all-start.2) | async-done | bytes 3670048 | tf_op jit(solution)/shard_map/all_to_all | solution.py:75
  69.9 8.2 %all-to-all-start = ((bf16[128,168,128]{2,1,0:T(8,128)(2,1)}), bf16[128,168,128]{2,1,0:T(8,128)(2,1)}, u32[]{:S(2)}, u32[]{:S(2)}) async-start(bf16[128,168,128]{2,1,0:T(8,128)(2,1)} %reshape.126), calls=%async_computation | async-start | bytes 11010048 | tf_op jit(solution)/shard_map/all_to_all | solution.py:75
  78.0 7.7 %reshape.131 = bf16[512,3584]{1,0:T(8,128)(2,1)} reshape(bf16[128,112,128]{2,1,0:T(8,128)(2,1)} %all-to-all-done.2) | data formatting | bytes 7340032 | tf_op jit(solution)/shard_map/reshape | solution.py:76
  85.7 9.5 %fusion.4 = f32[512,1024]{1,0:T(8,128)} fusion(bf16[512,3584]{1,0:T(8,128)(2,1)} %reshape.131, bf16[1,3584,1024]{2,1,0:T(8,128)(2,1)} %param.12), kind=kOutput, calls=%fused_computation.5 | convolution fusion | flops 3758096384 | bytes 13107200 | tf_op jit(solution)/shard_map/dot_general | solution.py:49
  95.2 16.7 %fusion.15 = bf16[512,3584]{1,0:T(8,128)(2,1)} fusion(bf16[1,1024,3584]{2,1,0:T(8,128)(2,1)} %param.13, f32[512,1024]{1,0:T(8,128)} %fusion.4, bf16[512,3584]{1,0:T(8,128)(2,1)} %reshape.131, bf16[1,3584,1024]{2,1,0:T(8,128)(2,1)} %param.11), kind=kOutput, calls=%fused_computation.15 | convolution fusion | flops 7521173504 | bytes 24117248 | tf_op jit(solution)/shard_map/dot_general | solution.py:51
  111.9 8.0 %reshape.132 = bf16[128,112,128]{2,1,0:T(8,128)(2,1)} reshape(bf16[512,3584]{1,0:T(8,128)(2,1)} %fusion.15) | data formatting | bytes 7340032 | tf_op jit(solution)/shard_map/reshape | solution.py:76
  119.8 23.7 %all-to-all-done = bf16[128,168,128]{2,1,0:T(8,128)(2,1)} async-done(((bf16[128,168,128]{2,1,0:T(8,128)(2,1)}), bf16[128,168,128]{2,1,0:T(8,128)(2,1)}, u32[]{:S(2)}, u32[]{:S(2)}) %all-to-all-start) | async-done | bytes 5505056 | tf_op jit(solution)/shard_map/all_to_all | solution.py:75
  143.5 6.9 %all-to-all-start.3 = ((bf16[128,112,128]{2,1,0:T(8,128)(2,1)}), bf16[128,112,128]{2,1,0:T(8,128)(2,1)}, u32[]{:S(2)}, u32[]{:S(2)}) async-start(bf16[128,112,128]{2,1,0:T(8,128)(2,1)} %reshape.132), calls=%async_computation.3 | async-start | bytes 7340032 | tf_op jit(solution)/shard_map/all_to_all | solution.py:77
  150.4 10.7 %reshape.127 = bf16[768,3584]{1,0:T(8,128)(2,1)} reshape(bf16[128,168,128]{2,1,0:T(8,128)(2,1)} %all-to-all-done) | data formatting | bytes 11010048 | tf_op jit(solution)/shard_map/reshape | solution.py:76
  161.1 10.9 %fusion.6 = f32[768,1024]{1,0:T(8,128)} fusion(bf16[768,3584]{1,0:T(8,128)(2,1)} %reshape.127, bf16[1,3584,1024]{2,1,0:T(8,128)(2,1)} %param.12), kind=kOutput, calls=%fused_computation.7 | convolution fusion | flops 5637144576 | bytes 15990784 | tf_op jit(solution)/shard_map/dot_general | solution.py:49
  172.0 20.0 %fusion.12 = bf16[768,3584]{1,0:T(8,128)(2,1)} fusion(bf16[1,1024,3584]{2,1,0:T(8,128)(2,1)} %param.13, f32[768,1024]{1,0:T(8,128)} %fusion.6, bf16[768,3584]{1,0:T(8,128)(2,1)} %reshape.127, bf16[1,3584,1024]{2,1,0:T(8,128)(2,1)} %param.11), kind=kOutput, calls=%fused_computation.14 | convolution fusion | flops 11281760256 | bytes 28835840 | tf_op jit(solution)/shard_map/dot_general | solution.py:51
  192.0 11.1 %reshape.128 = bf16[128,168,128]{2,1,0:T(8,128)(2,1)} reshape(bf16[768,3584]{1,0:T(8,128)(2,1)} %fusion.12) | data formatting | bytes 11010048 | tf_op jit(solution)/shard_map/reshape | solution.py:76
  203.1 10.2 %all-to-all-start.1 = ((bf16[128,168,128]{2,1,0:T(8,128)(2,1)}), bf16[128,168,128]{2,1,0:T(8,128)(2,1)}, u32[]{:S(2)}, u32[]{:S(2)}) async-start(bf16[128,168,128]{2,1,0:T(8,128)(2,1)} %reshape.128), calls=%async_computation.1 | async-start | bytes 11010048 | tf_op jit(solution)/shard_map/all_to_all | solution.py:77
  213.9 6.8 %gather_fusion = f32[1024]{0:T(1024)S(1)} fusion(f32[128,128]{1,0:T(8,128)S(1)} %fusion.33, s32[1024]{0:T(1024)S(1)} %reshape.134), kind=kCustom, calls=%fused_computation | custom fusion | bytes 16384 | tf_op jit(solution)/shard_map/jit(take_along_axis)/gather | solution.py:64
  221.5 1.0 select_reduce_fusion.1
  222.5 1.4 select_reduce_fusion
  223.9 7.7 %reshape.133 = bf16[512,3584]{1,0:T(8,128)(2,1)} reshape(bf16[128,112,128]{2,1,0:T(8,128)(2,1)} %all-to-all-done.3) | data formatting | bytes 7340032 | tf_op jit(solution)/shard_map/reshape | solution.py:78
  231.6 2.7 fusion.46
  234.3 44.4 %all-to-all-done.1 = bf16[128,168,128]{2,1,0:T(8,128)(2,1)} async-done(((bf16[128,168,128]{2,1,0:T(8,128)(2,1)}), bf16[128,168,128]{2,1,0:T(8,128)(2,1)}, u32[]{:S(2)}, u32[]{:S(2)}) %all-to-all-start.1) | async-done | bytes 5505056 | tf_op jit(solution)/shard_map/all_to_all | solution.py:77
  278.8 10.6 %reshape.129 = bf16[768,3584]{1,0:T(8,128)(2,1)} reshape(bf16[128,168,128]{2,1,0:T(8,128)(2,1)} %all-to-all-done.1) | data formatting | bytes 11010048 | tf_op jit(solution)/shard_map/reshape | solution.py:78
  289.4 3.6 %fusion.44 = f32[128,3584]{1,0:T(8,128)S(1)} fusion(bf16[768,3584]{1,0:T(8,128)(2,1)} %reshape.129, f32[128,768]{1,0:T(8,128)S(1)} %select_reduce_fusion), kind=kOutput, calls=%fused_computation.53 | convolution fusion | flops 704839680 | bytes 7733248 | tf_op jit(solution)/shard_map/dot_general | solution.py:42
  293.6 0.9 convolution_add_fusion.1
  294.5 1.1 copy-done.2
  295.6 1.7 fusion.19
  (36 shorter events, 3.9 us)
Async XLA Ops:
  0.0 3.7 %copy-start = (bf16[128,3584]{1,0:T(8,128)(2,1)S(1)}, bf16[128,3584]{1,0:T(8,128)(2,1)}, u32[]{:S(2)}) copy-start(bf16[128,3584]{1,0:T(8,128)(2,1)} %param.7) | copy-start | bytes 2752516
  14.6 55.3 %all-to-all-start.2 = ((bf16[128,112,128]{2,1,0:T(8,128)(2,1)}), bf16[128,112,128]{2,1,0:T(8,128)(2,1)}, u32[]{:S(2)}, u32[]{:S(2)}) async-start(bf16[128,112,128]{2,1,0:T(8,128)(2,1)} %reshape.130), calls=%async_computation.2 | async-start | bytes 7340032 | tf_op jit(solution)/shard_map/all_to_all | solution.py:75
  69.9 73.7 %all-to-all-start = ((bf16[128,168,128]{2,1,0:T(8,128)(2,1)}), bf16[128,168,128]{2,1,0:T(8,128)(2,1)}, u32[]{:S(2)}, u32[]{:S(2)}) async-start(bf16[128,168,128]{2,1,0:T(8,128)(2,1)} %reshape.126), calls=%async_computation | async-start | bytes 11010048 | tf_op jit(solution)/shard_map/all_to_all | solution.py:75
  143.5 59.6 %all-to-all-start.3 = ((bf16[128,112,128]{2,1,0:T(8,128)(2,1)}), bf16[128,112,128]{2,1,0:T(8,128)(2,1)}, u32[]{:S(2)}, u32[]{:S(2)}) async-start(bf16[128,112,128]{2,1,0:T(8,128)(2,1)} %reshape.132), calls=%async_computation.3 | async-start | bytes 7340032 | tf_op jit(solution)/shard_map/all_to_all | solution.py:77
  203.1 10.4 %copy-start.3 = (bf16[3584,128]{1,0:T(8,128)(2,1)S(1)}, bf16[3584,128]{1,0:T(8,128)(2,1)}, u32[]{:S(2)}) copy-start(bf16[3584,128]{1,0:T(8,128)(2,1)} %param.10) | copy-start | bytes 2752516
  203.1 75.7 %all-to-all-start.1 = ((bf16[128,168,128]{2,1,0:T(8,128)(2,1)}), bf16[128,168,128]{2,1,0:T(8,128)(2,1)}, u32[]{:S(2)}, u32[]{:S(2)}) async-start(bf16[128,168,128]{2,1,0:T(8,128)(2,1)} %reshape.128), calls=%async_computation.1 | async-start | bytes 11010048 | tf_op jit(solution)/shard_map/all_to_all | solution.py:77
  289.4 4.2 %copy-start.1 = (bf16[768,3584]{1,0:T(8,128)(2,1)S(1)}, bf16[768,3584]{1,0:T(8,128)(2,1)}, u32[]{:S(2)}) copy-start(bf16[768,3584]{1,0:T(8,128)(2,1)} %reshape.129) | copy-start | bytes 16515076
  293.6 2.0 copy-start.2

commit v2 on v1

--- a/solution.py
+++ b/solution.py
@@ -19,6 +19,10 @@
         return (cap_rows,)
     first = min(whole, key=lambda p: abs(2 * p - cap_rows) + (p < cap_rows - p))
     return (first, cap_rows - first)
+
+
+def wire_of(size, feat_width, experts_all):
+    return (experts_all, size * feat_width // LANES, LANES)
 
 
 def gather_piece(tokens, flat_ids, positions, start, size, experts_all):
@@ -68,15 +72,25 @@
     pieces = slot_pieces(cap_rows, feat_width)
     weights = 2.5 * picked / picked_total[:, None]
     mixed = jnp.zeros((tok_dev, feat_width), jnp.float32)
-    start = 0
-    for size in pieces:
-        wire = (experts_all, size * feat_width // LANES, LANES)
-        send_rows = gather_piece(tokens, flat_ids, positions, start, size, experts_all).reshape(wire)
-        received = lax.all_to_all(send_rows, ("node", "local"), split_axis=0, concat_axis=0, tiled=True)
-        produced = expert_rows(received.reshape(-1, feat_width), w_gate, w_up, w_down).reshape(wire)
-        returned = lax.all_to_all(produced, ("node", "local"), split_axis=0, concat_axis=0, tiled=True)
-        mixed = mixed + combine_piece(returned.reshape(-1, feat_width), weights, flat_ids, positions, start, size)
-        start += size
+    starts = [sum(pieces[:i]) for i in range(len(pieces))]
+    sent = [
+        gather_piece(tokens, flat_ids, positions, start, size, experts_all).reshape(wire_of(size, feat_width, experts_all))
+        for start, size in zip(starts, pieces)
+    ]
+    received = []
+    for i, send_rows in enumerate(sent):
+        if i:
+            received[-1], send_rows = lax.optimization_barrier((received[-1], send_rows))
+        received.append(lax.all_to_all(send_rows, ("node", "local"), split_axis=0, concat_axis=0, tiled=True))
+    returned = []
+    for i, (start, size) in enumerate(zip(starts, pieces)):
+        produced = expert_rows(received[i].reshape(-1, feat_width), w_gate, w_up, w_down).reshape(received[i].shape)
+        if i:
+            returned[-1], produced = lax.optimization_barrier((returned[-1], produced))
+        returned.append(lax.all_to_all(produced, ("node", "local"), split_axis=0, concat_axis=0, tiled=True))
+    for i, (start, size) in enumerate(zip(starts, pieces)):
+        rows = returned[i].reshape(-1, feat_width)
+        mixed = mixed + combine_piece(rows, weights, flat_ids, positions, start, size)
     return mixed.astype(jnp.bfloat16)
 
 

time: 302 us -> 301 us (level)
  transfers between devices with their start and end apart: 4 -> 4, of which waited for: 3 -> 3; matrix products, arithmetic and copies ran while one was open for 44% -> 45% of each run, Pallas kernels for 0% -> 0%
where the time goes in v2:
time: 301 us; the launch traced here: 295 us
  waiting for transfers between devices  95.4 us (32%)
  local copies, waits for them, and re-layouts  84.1 us (28%)
  matrix products  73.5 us (24%)
  starting transfers between devices  34.7 us (12%)
  other arithmetic  6.86 us (2%)
    all_to_all x2, waiting for transfers between devices, on_device(): lax.all_to_all(send_rows, ('node', 'local'), split_axis=0, concat_axis=0,...  53.6 us
    all_to_all x2, waiting for transfers between devices, on_device(): lax.all_to_all(produced, ('node', 'local'), split_axis=0, concat_axis=0,...  41.8 us
    dot_general x2, matrix products, expert_rows(): jnp.dot(hidden, w_down[0], preferred_element_type=jnp.float32)  36.7 us
    dot_general x2, matrix products, expert_rows(): up_part = jnp.dot(flat_rows, w_up[0], preferred_element_type=jnp.float32)  20.4 us
    reshape x2, local copies, waits for them, and re-layouts, on_device(): gather_piece(tokens, flat_ids, positions, start, size, experts_all)  19.1 us
    reshape x2, local copies, waits for them, and re-layouts, on_device(): expert_rows(received[i].reshape(-1, feat_width), w_gate, w_up, w_down)  19.1 us
    reshape x2, local copies, waits for them, and re-layouts, on_device(): received[i].reshape(-1, feat_width)  18.4 us
    reshape x2, local copies, waits for them, and re-layouts, on_device(): rows = returned[i].reshape(-1, feat_width)  18.3 us
  transfers between devices with their start and end apart: 4, of which 3 were waited for; matrix products, arithmetic and copies ran while one was open for 45% of the time, Pallas kernels for 0%

profile of v2, /device:TPU:14, one launch (start us, length us, event | category | flops | bytes accessed | tf_op | source)
XLA Modules:
  0.0 294.8 jit_solution(10270935410994027336)
XLA Ops:
  0.0 0.8 broadcast_multiply_fusion
  0.8 0.7 bitcast_or_fusion
  2.8 1.4 fusion.21
  4.2 4.0 %convolution_convert_fusion = bf16[768,3584]{1,0:T(8,128)(2,1)} fusion(pred[768,128]{1,0:T(8,128)(4,1)S(1)} %fusion.21, bf16[128,3584]{1,0:T(8,128)(2,1)S(1)} %copy-done), kind=kOutput, calls=%fused_computation.13 | convolution fusion | flops 707395584 | bytes 6520832 | tf_op jit(solution)/shard_map/dot_general | solution.py:34
  8.2 11.2 %reshape.126 = bf16[128,168,128]{2,1,0:T(8,128)(2,1)} reshape(bf16[768,3584]{1,0:T(8,128)(2,1)} %convolution_convert_fusion) | data formatting | bytes 11010048 | tf_op jit(solution)/shard_map/reshape | solution.py:77
  19.3 10.8 %all-to-all-start = ((bf16[128,168,128]{2,1,0:T(8,128)(2,1)}), bf16[128,168,128]{2,1,0:T(8,128)(2,1)}, u32[]{:S(2)}, u32[]{:S(2)}) async-start(bf16[128,168,128]{2,1,0:T(8,128)(2,1)} %reshape.126), calls=%async_computation | async-start | bytes 11010048 | tf_op jit(solution)/shard_map/all_to_all | solution.py:84
  30.1 0.9 fusion.26
  31.0 3.0 %convolution_convert_fusion.1 = bf16[512,3584]{1,0:T(8,128)(2,1)} fusion(pred[512,128]{1,0:T(8,128)(4,1)S(1)} %fusion.26, bf16[128,3584]{1,0:T(8,128)(2,1)S(1)} %copy-done), kind=kOutput, calls=%fused_computation.16 | convolution fusion | flops 471597056 | bytes 4653056 | tf_op jit(solution)/shard_map/dot_general | solution.py:34
  34.0 8.0 %reshape.127 = bf16[128,112,128]{2,1,0:T(8,128)(2,1)} reshape(bf16[512,3584]{1,0:T(8,128)(2,1)} %convolution_convert_fusion.1) | data formatting | bytes 7340032 | tf_op jit(solution)/shard_map/reshape | solution.py:77
  42.0 53.6 %all-to-all-done = bf16[128,168,128]{2,1,0:T(8,128)(2,1)} async-done(((bf16[128,168,128]{2,1,0:T(8,128)(2,1)}), bf16[128,168,128]{2,1,0:T(8,128)(2,1)}, u32[]{:S(2)}, u32[]{:S(2)}) %all-to-all-start) | async-done | bytes 5505056 | tf_op jit(solution)/shard_map/all_to_all | solution.py:84
  95.6 6.9 %all-to-all-start.2 = ((bf16[128,112,128]{2,1,0:T(8,128)(2,1)}), bf16[128,112,128]{2,1,0:T(8,128)(2,1)}, u32[]{:S(2)}, u32[]{:S(2)}) async-start(bf16[128,112,128]{2,1,0:T(8,128)(2,1)} %reshape.127), calls=%async_computation.2 | async-start | bytes 7340032 | tf_op jit(solution)/shard_map/all_to_all | solution.py:84
  102.5 10.7 %reshape.128 = bf16[768,3584]{1,0:T(8,128)(2,1)} reshape(bf16[128,168,128]{2,1,0:T(8,128)(2,1)} %all-to-all-done) | data formatting | bytes 11010048 | tf_op jit(solution)/shard_map/reshape | solution.py:87
  113.1 10.9 %fusion.6 = f32[768,1024]{1,0:T(8,128)} fusion(bf16[768,3584]{1,0:T(8,128)(2,1)} %reshape.128, bf16[1,3584,1024]{2,1,0:T(8,128)(2,1)} %param.12), kind=kOutput, calls=%fused_computation.7 | convolution fusion | flops 5637144576 | bytes 15990784 | tf_op jit(solution)/shard_map/dot_general | solution.py:53
  124.0 20.0 %fusion.12 = bf16[768,3584]{1,0:T(8,128)(2,1)} fusion(bf16[1,1024,3584]{2,1,0:T(8,128)(2,1)} %param.13, f32[768,1024]{1,0:T(8,128)} %fusion.6, bf16[768,3584]{1,0:T(8,128)(2,1)} %reshape.128, bf16[1,3584,1024]{2,1,0:T(8,128)(2,1)} %param.11), kind=kOutput, calls=%fused_computation.14 | convolution fusion | flops 11281760256 | bytes 28835840 | tf_op jit(solution)/shard_map/dot_general | solution.py:55
  144.1 11.2 %reshape.129 = bf16[128,168,128]{2,1,0:T(8,128)(2,1)} reshape(bf16[768,3584]{1,0:T(8,128)(2,1)} %fusion.12) | data formatting | bytes 11010048 | tf_op jit(solution)/shard_map/reshape | solution.py:87
  155.2 10.2 %all-to-all-start.1 = ((bf16[128,168,128]{2,1,0:T(8,128)(2,1)}), bf16[128,168,128]{2,1,0:T(8,128)(2,1)}, u32[]{:S(2)}, u32[]{:S(2)}) async-start(bf16[128,168,128]{2,1,0:T(8,128)(2,1)} %reshape.129), calls=%async_computation.1 | async-start | bytes 11010048 | tf_op jit(solution)/shard_map/all_to_all | solution.py:90
  165.4 7.7 %reshape.130 = bf16[512,3584]{1,0:T(8,128)(2,1)} reshape(bf16[128,112,128]{2,1,0:T(8,128)(2,1)} %all-to-all-done.2) | data formatting | bytes 7340032 | tf_op jit(solution)/shard_map/reshape | solution.py:87
  173.1 9.5 %fusion.4 = f32[512,1024]{1,0:T(8,128)} fusion(bf16[512,3584]{1,0:T(8,128)(2,1)} %reshape.130, bf16[1,3584,1024]{2,1,0:T(8,128)(2,1)} %param.12), kind=kOutput, calls=%fused_computation.5 | convolution fusion | flops 3758096384 | bytes 13107200 | tf_op jit(solution)/shard_map/dot_general | solution.py:53
  182.6 16.7 %fusion.15 = bf16[512,3584]{1,0:T(8,128)(2,1)} fusion(bf16[1,1024,3584]{2,1,0:T(8,128)(2,1)} %param.13, f32[512,1024]{1,0:T(8,128)} %fusion.4, bf16[512,3584]{1,0:T(8,128)(2,1)} %reshape.130, bf16[1,3584,1024]{2,1,0:T(8,128)(2,1)} %param.11), kind=kOutput, calls=%fused_computation.15 | convolution fusion | flops 7521173504 | bytes 24117248 | tf_op jit(solution)/shard_map/dot_general | solution.py:55
  199.3 8.0 %reshape.131 = bf16[128,112,128]{2,1,0:T(8,128)(2,1)} reshape(bf16[512,3584]{1,0:T(8,128)(2,1)} %fusion.15) | data formatting | bytes 7340032 | tf_op jit(solution)/shard_map/reshape | solution.py:87
  207.2 23.6 %all-to-all-done.1 = bf16[128,168,128]{2,1,0:T(8,128)(2,1)} async-done(((bf16[128,168,128]{2,1,0:T(8,128)(2,1)}), bf16[128,168,128]{2,1,0:T(8,128)(2,1)}, u32[]{:S(2)}, u32[]{:S(2)}) %all-to-all-start.1) | async-done | bytes 5505056 | tf_op jit(solution)/shard_map/all_to_all | solution.py:90
  230.9 6.9 %all-to-all-start.3 = ((bf16[128,112,128]{2,1,0:T(8,128)(2,1)}), bf16[128,112,128]{2,1,0:T(8,128)(2,1)}, u32[]{:S(2)}, u32[]{:S(2)}) async-start(bf16[128,112,128]{2,1,0:T(8,128)(2,1)} %reshape.131), calls=%async_computation.3 | async-start | bytes 7340032 | tf_op jit(solution)/shard_map/all_to_all | solution.py:90
  238.6 6.8 %gather_fusion = f32[1024]{0:T(1024)S(1)} fusion(f32[128,128]{1,0:T(8,128)S(1)} %fusion.33, s32[1024]{0:T(1024)S(1)} %reshape.134), kind=kCustom, calls=%fused_computation | custom fusion | bytes 16384 | tf_op jit(solution)/shard_map/jit(take_along_axis)/gather | solution.py:68
  245.9 1.0 select_reduce_fusion.1
  247.0 1.4 select_reduce_fusion
  248.4 10.7 %reshape.132 = bf16[768,3584]{1,0:T(8,128)(2,1)} reshape(bf16[128,168,128]{2,1,0:T(8,128)(2,1)} %all-to-all-done.1) | data formatting | bytes 11010048 | tf_op jit(solution)/shard_map/reshape | solution.py:92
  259.1 3.6 %fusion.44 = f32[128,3584]{1,0:T(8,128)S(1)} fusion(bf16[768,3584]{1,0:T(8,128)(2,1)} %reshape.132, f32[128,768]{1,0:T(8,128)S(1)} %select_reduce_fusion), kind=kOutput, calls=%fused_computation.53 | convolution fusion | flops 704839680 | bytes 7733248 | tf_op jit(solution)/shard_map/dot_general | solution.py:46
  263.2 0.9 convolution_add_fusion.1
  264.1 18.1 %all-to-all-done.3 = bf16[128,112,128]{2,1,0:T(8,128)(2,1)} async-done(((bf16[128,112,128]{2,1,0:T(8,128)(2,1)}), bf16[128,112,128]{2,1,0:T(8,128)(2,1)}, u32[]{:S(2)}, u32[]{:S(2)}) %all-to-all-start.3) | async-done | bytes 3670048 | tf_op jit(solution)/shard_map/all_to_all | solution.py:90
  282.3 7.7 %reshape.133 = bf16[512,3584]{1,0:T(8,128)(2,1)} reshape(bf16[128,112,128]{2,1,0:T(8,128)(2,1)} %all-to-all-done.3) | data formatting | bytes 7340032 | tf_op jit(solution)/shard_map/reshape | solution.py:92
  290.0 2.8 fusion.46
  293.1 1.7 fusion.19
  (36 shorter events, 3.5 us)
Async XLA Ops:
  0.0 4.2 %copy-start = (bf16[128,3584]{1,0:T(8,128)(2,1)S(1)}, bf16[128,3584]{1,0:T(8,128)(2,1)}, u32[]{:S(2)}) copy-start(bf16[128,3584]{1,0:T(8,128)(2,1)} %param.7) | copy-start | bytes 2752516
  19.3 76.3 %all-to-all-start = ((bf16[128,168,128]{2,1,0:T(8,128)(2,1)}), bf16[128,168,128]{2,1,0:T(8,128)(2,1)}, u32[]{:S(2)}, u32[]{:S(2)}) async-start(bf16[128,168,128]{2,1,0:T(8,128)(2,1)} %reshape.126), calls=%async_computation | async-start | bytes 11010048 | tf_op jit(solution)/shard_map/all_to_all | solution.py:84
  95.6 59.6 %all-to-all-start.2 = ((bf16[128,112,128]{2,1,0:T(8,128)(2,1)}), bf16[128,112,128]{2,1,0:T(8,128)(2,1)}, u32[]{:S(2)}, u32[]{:S(2)}) async-start(bf16[128,112,128]{2,1,0:T(8,128)(2,1)} %reshape.127), calls=%async_computation.2 | async-start | bytes 7340032 | tf_op jit(solution)/shard_map/all_to_all | solution.py:84
  155.2 75.7 %all-to-all-start.1 = ((bf16[128,168,128]{2,1,0:T(8,128)(2,1)}), bf16[128,168,128]{2,1,0:T(8,128)(2,1)}, u32[]{:S(2)}, u32[]{:S(2)}) async-start(bf16[128,168,128]{2,1,0:T(8,128)(2,1)} %reshape.129), calls=%async_computation.1 | async-start | bytes 11010048 | tf_op jit(solution)/shard_map/all_to_all | solution.py:90
  207.2 31.0 %copy-start.3 = (bf16[3584,128]{1,0:T(8,128)(2,1)S(1)}, bf16[3584,128]{1,0:T(8,128)(2,1)}, u32[]{:S(2)}) copy-start(bf16[3584,128]{1,0:T(8,128)(2,1)} %param.10) | copy-start | bytes 2752516
  230.9 51.4 %all-to-all-start.3 = ((bf16[128,112,128]{2,1,0:T(8,128)(2,1)}), bf16[128,112,128]{2,1,0:T(8,128)(2,1)}, u32[]{:S(2)}, u32[]{:S(2)}) async-start(bf16[128,112,128]{2,1,0:T(8,128)(2,1)} %reshape.131), calls=%async_computation.3 | async-start | bytes 7340032 | tf_op jit(solution)/shard_map/all_to_all | solution.py:90
  259.1 4.2 %copy-start.1 = (bf16[768,3584]{1,0:T(8,128)(2,1)S(1)}, bf16[768,3584]{1,0:T(8,128)(2,1)}, u32[]{:S(2)}) copy-start(bf16[768,3584]{1,0:T(8,128)(2,1)} %reshape.132) | copy-start | bytes 16515076
  290.0 3.1 %copy-start.2 = (bf16[512,3584]{1,0:T(8,128)(2,1)S(1)}, bf16[512,3584]{1,0:T(8,128)(2,1)}, u32[]{:S(2)}) copy-start(bf16[512,3584]{1,0:T(8,128)(2,1)} %reshape.133) | copy-start | bytes 11010052

commit v3 on v2

--- a/solution.py
+++ b/solution.py
@@ -13,15 +13,16 @@
 
 
 def slot_pieces(cap_rows, feat_width):
-    tile_rows = 8 * LANES // feat_width if feat_width < 8 * LANES else 1
-    whole = [p for p in range(1, cap_rows) if (p * feat_width // LANES) % 8 == 0 and ((cap_rows - p) * feat_width // LANES) % 8 == 0]
-    if not whole or cap_rows * feat_width % LANES:
-        return (cap_rows,)
-    first = min(whole, key=lambda p: abs(2 * p - cap_rows) + (p < cap_rows - p))
-    return (first, cap_rows - first)
+    first = cap_rows // 8 * 8
+    rest = cap_rows - first
+    if first and rest and (rest * feat_width // LANES) % 8 == 0 and feat_width % LANES == 0:
+        return (first, rest)
+    return (cap_rows,)
 
 
 def wire_of(size, feat_width, experts_all):
+    if size % 8 == 0:
+        return (experts_all, size, feat_width)
     return (experts_all, size * feat_width // LANES, LANES)
 
 

time: 301 us -> 289 us (0.960)
  local copies, waits for them, and re-layouts: 84.1 us -> 23.9 us
  waiting for transfers between devices: 95.4 us -> 148 us
    all_to_all x2, waiting for transfers between devices: 53.6 us -> 83.5 us  [on_device(): lax.all_to_all(send_rows, ('node', 'local'), split_axis=0, concat_axis=0,...]
    all_to_all x2, waiting for transfers between devices: 41.8 us -> 64.9 us  [on_device(): lax.all_to_all(produced, ('node', 'local'), split_axis=0, concat_axis=0,...]
    dot_general x0 -> x2, matrix products: none -> 19.7 us  [expert_rows(): jnp.dot(flat_rows, w_gate[0], preferred_element_type=jnp.float32)]
    dot_general x2, matrix products: 36.7 us -> 20.6 us  [expert_rows(): jnp.dot(hidden, w_down[0], preferred_element_type=jnp.float32)]
    reshape x2 -> x1, local copies, waits for them, and re-layouts: 19.1 us -> 3.28 us  [on_device(): gather_piece(tokens, flat_ids, positions, start, size, experts_all)]
    reshape x2 -> x1, local copies, waits for them, and re-layouts: 18.4 us -> 2.95 us  [on_device(): received[i].reshape(-1, feat_width)]
    reshape x2 -> x1, local copies, waits for them, and re-layouts: 18.3 us -> 3.6 us  [on_device(): rows = returned[i].reshape(-1, feat_width)]
    reshape x2 -> x1, local copies, waits for them, and re-layouts: 19.1 us -> 4.68 us  [on_device(): expert_rows(received[i].reshape(-1, feat_width), w_gate, w_up, w_down)]
  transfers between devices with their start and end apart: 4 -> 4, of which waited for: 3 -> 3; matrix products, arithmetic and copies ran while one was open for 45% -> 30% of each run, Pallas kernels for 0% -> 0%
where the time goes in v3:
time: 289 us; the launch traced here: 284 us
  waiting for transfers between devices  148 us (51%)
  matrix products  70.6 us (24%)
  starting transfers between devices  34.1 us (12%)
  local copies, waits for them, and re-layouts  23.9 us (8%)
  other arithmetic  7.06 us (2%)
    all_to_all x2, waiting for transfers between devices, on_device(): lax.all_to_all(send_rows, ('node', 'local'), split_axis=0, concat_axis=0,...  83.5 us
    all_to_all x2, waiting for transfers between devices, on_device(): lax.all_to_all(produced, ('node', 'local'), split_axis=0, concat_axis=0,...  64.9 us
    dot_general x2, matrix products, expert_rows(): jnp.dot(hidden, w_down[0], preferred_element_type=jnp.float32)  20.6 us
    dot_general x2, matrix products, expert_rows(): jnp.dot(flat_rows, w_gate[0], preferred_element_type=jnp.float32)  19.7 us
    all_to_all x2, starting transfers between devices, on_device(): lax.all_to_all(send_rows, ('node', 'local'), split_axis=0, concat_axis=0,...  17.1 us
    all_to_all x2, starting transfers between devices, on_device(): lax.all_to_all(produced, ('node', 'local'), split_axis=0, concat_axis=0,...  17 us
    dot_general x1, matrix products, expert_rows(): up_part = jnp.dot(flat_rows, w_up[0], preferred_element_type=jnp.float32)  11.4 us
    gather x5, local copies, waits for them, and re-layouts, on_device(): picked = jnp.take_along_axis(affinity, expert_ids, axis=1)  7.12 us
  transfers between devices with their start and end apart: 4, of which 3 were waited for; matrix products, arithmetic and copies ran while one was open for 30% of the time, Pallas kernels for 0%

profile of v3, /device:TPU:14, one launch (start us, length us, event | category | flops | bytes accessed | tf_op | source)
XLA Modules:
  0.0 284.2 jit_solution(1135799743829471264)
XLA Ops:
  0.0 0.8 broadcast_multiply_fusion
  0.8 0.7 bitcast_or_fusion
  2.3 0.4 fusion.50
  2.8 1.9 fusion.30
  4.7 5.0 %fusion.17 = bf16[128,8,3584]{2,1,0:T(8,128)(2,1)} fusion(pred[1024,128]{1,0:T(8,128)(4,1)S(1)} %fusion.30, bf16[128,3584]{1,0:T(8,128)(2,1)S(1)} %copy-done), kind=kOutput, calls=%fused_computation.20 | convolution fusion | flops 943194112 | bytes 8388608 | tf_op jit(solution)/shard_map/dot_general | solution.py:35
  9.7 10.8 %all-to-all-start = ((bf16[128,8,3584]{2,1,0:T(8,128)(2,1)}), bf16[128,8,3584]{2,1,0:T(8,128)(2,1)}, u32[]{:S(2)}, u32[]{:S(2)}) async-start(bf16[128,8,3584]{2,1,0:T(8,128)(2,1)} %fusion.17), calls=%async_computation | async-start | bytes 14680064 | tf_op jit(solution)/shard_map/all_to_all | solution.py:85
  20.5 0.4 fusion.44
  20.8 0.6 convolution_convert_fusion.2
  21.5 3.3 %reshape.127 = bf16[128,56,128]{2,1,0:T(8,128)(2,1)} reshape(bf16[256,3584]{1,0:T(8,128)(2,1)S(1)} %convolution_convert_fusion.2) | data formatting | bytes 3670016 | tf_op jit(solution)/shard_map/reshape | solution.py:78
  24.7 83.5 %all-to-all-done = bf16[128,8,3584]{2,1,0:T(8,128)(2,1)} async-done(((bf16[128,8,3584]{2,1,0:T(8,128)(2,1)}), bf16[128,8,3584]{2,1,0:T(8,128)(2,1)}, u32[]{:S(2)}, u32[]{:S(2)}) %all-to-all-start) | async-done | bytes 7340064 | tf_op jit(solution)/shard_map/all_to_all | solution.py:85
  108.2 6.3 %all-to-all-start.2 = ((bf16[128,56,128]{2,1,0:T(8,128)(2,1)}), bf16[128,56,128]{2,1,0:T(8,128)(2,1)S(1)}, u32[]{:S(2)}, u32[]{:S(2)}) async-start(bf16[128,56,128]{2,1,0:T(8,128)(2,1)} %reshape.127), calls=%async_computation.2 | async-start | bytes 3670016 | tf_op jit(solution)/shard_map/all_to_all | solution.py:85
  114.6 11.4 %fusion.9 = f32[1024,1024]{1,0:T(8,128)S(1)} fusion(bf16[1,3584,1024]{2,1,0:T(8,128)(2,1)} %param.12, bf16[128,8,3584]{2,1,0:T(8,128)(2,1)} %all-to-all-done), kind=kOutput, calls=%fused_computation.12 | convolution fusion | flops 7516192768 | bytes 18874368 | tf_op jit(solution)/shard_map/dot_general | solution.py:54
  125.9 12.9 %multiply_convert_fusion = bf16[1024,1024]{1,0:T(8,128)(2,1)S(1)} fusion(f32[1024,1024]{1,0:T(8,128)S(1)} %fusion.9, bf16[1,3584,1024]{2,1,0:T(8,128)(2,1)} %param.11, bf16[128,8,3584]{2,1,0:T(8,128)(2,1)} %all-to-all-done), kind=kOutput, calls=%fused_computation.28 | convolution fusion | flops 7522484224 | bytes 20971520 | tf_op jit(solution)/shard_map/dot_general | solution.py:53
  138.9 9.8 %fusion.18 = bf16[128,8,3584]{2,1,0:T(8,128)(2,1)} fusion(bf16[1024,1024]{1,0:T(8,128)(2,1)S(1)} %multiply_convert_fusion, bf16[1,1024,3584]{2,1,0:T(8,128)(2,1)S(1)} %bitcast.73), kind=kOutput, calls=%fused_computation.21 | convolution fusion | flops 7519862784 | bytes 16777216 | tf_op jit(solution)/shard_map/dot_general | solution.py:56
  148.7 10.2 %all-to-all-start.1 = ((bf16[128,8,3584]{2,1,0:T(8,128)(2,1)}), bf16[128,8,3584]{2,1,0:T(8,128)(2,1)}, u32[]{:S(2)}, u32[]{:S(2)}) async-start(bf16[128,8,3584]{2,1,0:T(8,128)(2,1)} %fusion.18), calls=%async_computation.1 | async-start | bytes 14680064 | tf_op jit(solution)/shard_map/all_to_all | solution.py:91
  159.3 1.6 fusion.43
  160.9 6.8 %gather_fusion = f32[1024]{0:T(1024)S(1)} fusion(f32[128,128]{1,0:T(8,128)S(1)} %fusion.43, s32[1024]{0:T(1024)S(1)} %reshape.134), kind=kCustom, calls=%fused_computation | custom fusion | bytes 16384 | tf_op jit(solution)/shard_map/jit(take_along_axis)/gather | solution.py:69
  167.9 3.0 %reshape.130 = bf16[256,3584]{1,0:T(8,128)(2,1)} reshape(bf16[128,56,128]{2,1,0:T(8,128)(2,1)S(1)} %all-to-all-done.2) | data formatting | bytes 3670016 | tf_op jit(solution)/shard_map/reshape | solution.py:88
  170.8 6.8 %fusion.11 = f32[256,1024]{1,0:T(8,128)} fusion(bf16[256,3584]{1,0:T(8,128)(2,1)} %reshape.130, bf16[1,3584,1024]{2,1,0:T(8,128)(2,1)} %param.11), kind=kOutput, calls=%fused_computation.14 | convolution fusion | flops 1879048192 | bytes 10223616 | tf_op jit(solution)/shard_map/dot_general | solution.py:53
  177.6 10.8 %fusion.21 = bf16[256,3584]{1,0:T(8,128)(2,1)} fusion(bf16[1,1024,3584]{2,1,0:T(8,128)(2,1)} %param.13, bf16[256,3584]{1,0:T(8,128)(2,1)S(1)} %copy-done.2, bf16[1,3584,1024]{2,1,0:T(8,128)(2,1)} %param.12, f32[256,1024]{1,0:T(8,128)} %fusion.11), kind=kOutput, calls=%fused_computation.22 | convolution fusion | flops 3760586752 | bytes 19398656 | tf_op jit(solution)/shard_map/dot_general | solution.py:56
  188.4 4.7 %reshape.131 = bf16[128,56,128]{2,1,0:T(8,128)(2,1)} reshape(bf16[256,3584]{1,0:T(8,128)(2,1)} %fusion.21) | data formatting | bytes 3670016 | tf_op jit(solution)/shard_map/reshape | solution.py:88
  193.1 53.6 %all-to-all-done.1 = bf16[128,8,3584]{2,1,0:T(8,128)(2,1)} async-done(((bf16[128,8,3584]{2,1,0:T(8,128)(2,1)}), bf16[128,8,3584]{2,1,0:T(8,128)(2,1)}, u32[]{:S(2)}, u32[]{:S(2)}) %all-to-all-start.1) | async-done | bytes 7340064 | tf_op jit(solution)/shard_map/all_to_all | solution.py:91
  246.7 6.8 %all-to-all-start.3 = ((bf16[128,56,128]{2,1,0:T(8,128)(2,1)}), bf16[128,56,128]{2,1,0:T(8,128)(2,1)}, u32[]{:S(2)}, u32[]{:S(2)}) async-start(bf16[128,56,128]{2,1,0:T(8,128)(2,1)} %reshape.131), calls=%async_computation.3 | async-start | bytes 3670016 | tf_op jit(solution)/shard_map/all_to_all | solution.py:91
  253.9 0.8 select_reduce_fusion.1
  254.7 1.8 select_reduce_fusion
  256.5 4.2 %fusion = f32[128,3584]{1,0:T(8,128)S(1)} fusion(bf16[128,8,3584]{2,1,0:T(8,128)(2,1)} %all-to-all-done.1, f32[128,1024]{1,0:T(8,128)S(1)} %select_reduce_fusion), kind=kOutput, calls=%fused_computation.3 | convolution fusion | flops 939917312 | bytes 9699328 | tf_op jit(solution)/shard_map/dot_general | solution.py:47
  260.7 5.6 %fusion.25 = f32[128,3584]{1,0:T(8,128)} fusion(f32[128,3584]{1,0:T(8,128)S(1)} %fusion, bf16[128,8,3584]{2,1,0:T(8,128)(2,1)} %all-to-all-done.1, f32[128,1024]{1,0:T(8,128)S(1)} %select_reduce_fusion), kind=kOutput, calls=%fused_computation.26 | convolution fusion | flops 940244992 | bytes 11534336 | tf_op jit(solution)/shard_map/dot_general | solution.py:47
  266.3 11.3 %all-to-all-done.3 = bf16[128,56,128]{2,1,0:T(8,128)(2,1)} async-done(((bf16[128,56,128]{2,1,0:T(8,128)(2,1)}), bf16[128,56,128]{2,1,0:T(8,128)(2,1)}, u32[]{:S(2)}, u32[]{:S(2)}) %all-to-all-start.3) | async-done | bytes 1835040 | tf_op jit(solution)/shard_map/all_to_all | solution.py:91
  277.6 3.6 %reshape.133 = bf16[256,3584]{1,0:T(8,128)(2,1)S(1)} reshape(bf16[128,56,128]{2,1,0:T(8,128)(2,1)} %all-to-all-done.3) | data formatting | bytes 3670016 | tf_op jit(solution)/shard_map/reshape | solution.py:93
  281.2 0.4 fusion.58
  281.7 1.1 copy-done.1
  282.7 1.5 fusion.28
  (36 shorter events, 1.8 us)
Async XLA Ops:
  0.0 4.7 %copy-start = (bf16[128,3584]{1,0:T(8,128)(2,1)S(1)}, bf16[128,3584]{1,0:T(8,128)(2,1)}, u32[]{:S(2)}) copy-start(bf16[128,3584]{1,0:T(8,128)(2,1)} %param.7) | copy-start | bytes 2752516
  9.7 98.5 %all-to-all-start = ((bf16[128,8,3584]{2,1,0:T(8,128)(2,1)}), bf16[128,8,3584]{2,1,0:T(8,128)(2,1)}, u32[]{:S(2)}, u32[]{:S(2)}) async-start(bf16[128,8,3584]{2,1,0:T(8,128)(2,1)} %fusion.17), calls=%async_computation | async-start | bytes 14680064 | tf_op jit(solution)/shard_map/all_to_all | solution.py:85
  108.2 40.5 %all-to-all-start.2 = ((bf16[128,56,128]{2,1,0:T(8,128)(2,1)}), bf16[128,56,128]{2,1,0:T(8,128)(2,1)S(1)}, u32[]{:S(2)}, u32[]{:S(2)}) async-start(bf16[128,56,128]{2,1,0:T(8,128)(2,1)} %reshape.127), calls=%async_computation.2 | async-start | bytes 3670016 | tf_op jit(solution)/shard_map/all_to_all | solution.py:85
  114.5 24.3 %slice-start = ((s8[7340032]{0:T(1024)(128)(4,1)}), s8[4194304]{0:T(1024)(128)(4,1)S(1)}, s32[]{:S(2)}) async-start(s8[7340032]{0:T(1024)(128)(4,1)} %bitcast.72), calls=%async_computation.4 | async-start | bytes 8388608
  125.9 12.9 %slice-start.1 = ((s8[7340032]{0:T(1024)(128)(4,1)}), s8[3145728]{0:T(1024)(128)(4,1)S(1)}, s32[]{:S(2)}) async-start(s8[7340032]{0:T(1024)(128)(4,1)} %bitcast.72), calls=%async_computation.5 | async-start | bytes 6291456
  148.7 97.9 %all-to-all-start.1 = ((bf16[128,8,3584]{2,1,0:T(8,128)(2,1)}), bf16[128,8,3584]{2,1,0:T(8,128)(2,1)}, u32[]{:S(2)}, u32[]{:S(2)}) async-start(bf16[128,8,3584]{2,1,0:T(8,128)(2,1)} %fusion.18), calls=%async_computation.1 | async-start | bytes 14680064 | tf_op jit(solution)/shard_map/all_to_all | solution.py:91
  170.8 6.8 %copy-start.2 = (bf16[256,3584]{1,0:T(8,128)(2,1)S(1)}, bf16[256,3584]{1,0:T(8,128)(2,1)}, u32[]{:S(2)}) copy-start(bf16[256,3584]{1,0:T(8,128)(2,1)} %reshape.130) | copy-start | bytes 5505028
  246.7 31.0 %all-to-all-start.3 = ((bf16[128,56,128]{2,1,0:T(8,128)(2,1)}), bf16[128,56,128]{2,1,0:T(8,128)(2,1)}, u32[]{:S(2)}, u32[]{:S(2)}) async-start(bf16[128,56,128]{2,1,0:T(8,128)(2,1)} %reshape.131), calls=%async_computation.3 | async-start | bytes 3670016 | tf_op jit(solution)/shard_map/all_to_all | solution.py:91
  281.2 1.5 copy-start.1

commit v4 on v3

--- a/solution.py
+++ b/solution.py
@@ -16,7 +16,7 @@
     first = cap_rows // 8 * 8
     rest = cap_rows - first
     if first and rest and (rest * feat_width // LANES) % 8 == 0 and feat_width % LANES == 0:
-        return (first, rest)
+        return (rest, first)
     return (cap_rows,)
 
 

time: 289 us -> 289 us (level); the launches traced: 284 us -> 289 us
  waiting for transfers between devices: 148 us -> 151 us
    all_to_all x2, waiting for transfers between devices: 64.9 us -> 70.5 us  [on_device(): lax.all_to_all(produced, ('node', 'local'), split_axis=0, concat_axis=0,...]
    all_to_all x2, waiting for transfers between devices: 83.5 us -> 80 us  [on_device(): lax.all_to_all(send_rows, ('node', 'local'), split_axis=0, concat_axis=0,...]
  transfers between devices with their start and end apart: 4 -> 4, of which waited for: 3 -> 3; matrix products, arithmetic and copies ran while one was open for 30% -> 29% of each run, Pallas kernels for 0% -> 0%
where the time goes in v4:
time: 289 us
  waiting for transfers between devices  151 us (52%)
  matrix products  70.7 us (24%)
  starting transfers between devices  35.8 us (12%)
  local copies, waits for them, and re-layouts  24.1 us (8%)
  other arithmetic  7.06 us (2%)
    all_to_all x2, waiting for transfers between devices, on_device(): lax.all_to_all(send_rows, ('node', 'local'), split_axis=0, concat_axis=0,...  80 us
    all_to_all x2, waiting for transfers between devices, on_device(): lax.all_to_all(produced, ('node', 'local'), split_axis=0, concat_axis=0,...  70.5 us
    dot_general x2, matrix products, expert_rows(): jnp.dot(hidden, w_down[0], preferred_element_type=jnp.float32)  20.6 us
    dot_general x2, matrix products, expert_rows(): jnp.dot(flat_rows, w_gate[0], preferred_element_type=jnp.float32)  19.7 us
    all_to_all x2, starting transfers between devices, on_device(): lax.all_to_all(send_rows, ('node', 'local'), split_axis=0, concat_axis=0,...  19.2 us
    all_to_all x2, starting transfers between devices, on_device(): lax.all_to_all(produced, ('node', 'local'), split_axis=0, concat_axis=0,...  16.6 us
    dot_general x1, matrix products, expert_rows(): up_part = jnp.dot(flat_rows, w_up[0], preferred_element_type=jnp.float32)  11.4 us
    gather x5, local copies, waits for them, and re-layouts, on_device(): picked = jnp.take_along_axis(affinity, expert_ids, axis=1)  7.12 us
  transfers between devices with their start and end apart: 4, of which 3 were waited for; matrix products, arithmetic and copies ran while one was open for 29% of the time, Pallas kernels for 0%

profile of v4, /device:TPU:14, one launch (start us, length us, event | category | flops | bytes accessed | tf_op | source)
XLA Modules:
  0.0 288.5 jit_solution(17896856888021818071)
XLA Ops:
  0.0 0.8 broadcast_multiply_fusion
  0.8 0.7 bitcast_or_fusion
  2.3 0.4 fusion.50
  2.8 0.4 fusion.45
  3.2 0.6 convolution_convert_fusion.2
  3.8 3.3 %reshape.126 = bf16[128,56,128]{2,1,0:T(8,128)(2,1)} reshape(bf16[256,3584]{1,0:T(8,128)(2,1)S(1)} %convolution_convert_fusion.2) | data formatting | bytes 3670016 | tf_op jit(solution)/shard_map/reshape | solution.py:78
  7.1 10.4 %all-to-all-start = ((bf16[128,56,128]{2,1,0:T(8,128)(2,1)}), bf16[128,56,128]{2,1,0:T(8,128)(2,1)S(1)}, u32[]{:S(2)}, u32[]{:S(2)}) async-start(bf16[128,56,128]{2,1,0:T(8,128)(2,1)} %reshape.126), calls=%async_computation | async-start | bytes 3670016 | tf_op jit(solution)/shard_map/all_to_all | solution.py:85
  17.5 1.9 fusion.29
  19.4 5.0 %fusion.17 = bf16[128,8,3584]{2,1,0:T(8,128)(2,1)} fusion(pred[1024,128]{1,0:T(8,128)(4,1)S(1)} %fusion.29, bf16[128,3584]{1,0:T(8,128)(2,1)S(1)} %copy-done), kind=kOutput, calls=%fused_computation.20 | convolution fusion | flops 943194112 | bytes 8388608 | tf_op jit(solution)/shard_map/dot_general | solution.py:35
  24.4 17.5 %all-to-all-done = bf16[128,56,128]{2,1,0:T(8,128)(2,1)S(1)} async-done(((bf16[128,56,128]{2,1,0:T(8,128)(2,1)}), bf16[128,56,128]{2,1,0:T(8,128)(2,1)S(1)}, u32[]{:S(2)}, u32[]{:S(2)}) %all-to-all-start) | async-done | bytes 1835040 | tf_op jit(solution)/shard_map/all_to_all | solution.py:85
  41.9 8.9 %all-to-all-start.2 = ((bf16[128,8,3584]{2,1,0:T(8,128)(2,1)}), bf16[128,8,3584]{2,1,0:T(8,128)(2,1)}, u32[]{:S(2)}, u32[]{:S(2)}) async-start(bf16[128,8,3584]{2,1,0:T(8,128)(2,1)} %fusion.17), calls=%async_computation.2 | async-start | bytes 14680064 | tf_op jit(solution)/shard_map/all_to_all | solution.py:85
  50.7 3.0 %reshape.128 = bf16[256,3584]{1,0:T(8,128)(2,1)} reshape(bf16[128,56,128]{2,1,0:T(8,128)(2,1)S(1)} %all-to-all-done) | data formatting | bytes 3670016 | tf_op jit(solution)/shard_map/reshape | solution.py:88
  53.7 6.8 %fusion.15 = f32[256,1024]{1,0:T(8,128)} fusion(bf16[256,3584]{1,0:T(8,128)(2,1)} %reshape.128, bf16[1,3584,1024]{2,1,0:T(8,128)(2,1)} %param.11), kind=kOutput, calls=%fused_computation.18 | convolution fusion | flops 1879048192 | bytes 10223616 | tf_op jit(solution)/shard_map/dot_general | solution.py:53
  60.5 10.8 %fusion.21 = bf16[256,3584]{1,0:T(8,128)(2,1)} fusion(bf16[1,1024,3584]{2,1,0:T(8,128)(2,1)} %param.13, bf16[256,3584]{1,0:T(8,128)(2,1)S(1)} %copy-done.3, bf16[1,3584,1024]{2,1,0:T(8,128)(2,1)} %param.12, f32[256,1024]{1,0:T(8,128)} %fusion.15), kind=kOutput, calls=%fused_computation.22 | convolution fusion | flops 3760586752 | bytes 19398656 | tf_op jit(solution)/shard_map/dot_general | solution.py:56
  71.3 4.7 %reshape.129 = bf16[128,56,128]{2,1,0:T(8,128)(2,1)} reshape(bf16[256,3584]{1,0:T(8,128)(2,1)} %fusion.21) | data formatting | bytes 3670016 | tf_op jit(solution)/shard_map/reshape | solution.py:88
  76.0 62.6 %all-to-all-done.2 = bf16[128,8,3584]{2,1,0:T(8,128)(2,1)} async-done(((bf16[128,8,3584]{2,1,0:T(8,128)(2,1)}), bf16[128,8,3584]{2,1,0:T(8,128)(2,1)}, u32[]{:S(2)}, u32[]{:S(2)}) %all-to-all-start.2) | async-done | bytes 7340064 | tf_op jit(solution)/shard_map/all_to_all | solution.py:85
  138.5 6.4 %all-to-all-start.1 = ((bf16[128,56,128]{2,1,0:T(8,128)(2,1)}), bf16[128,56,128]{2,1,0:T(8,128)(2,1)S(1)}, u32[]{:S(2)}, u32[]{:S(2)}) async-start(bf16[128,56,128]{2,1,0:T(8,128)(2,1)} %reshape.129), calls=%async_computation.1 | async-start | bytes 3670016 | tf_op jit(solution)/shard_map/all_to_all | solution.py:91
  145.0 11.4 %fusion.4 = f32[1024,1024]{1,0:T(8,128)S(1)} fusion(bf16[128,8,3584]{2,1,0:T(8,128)(2,1)} %all-to-all-done.2, bf16[1,3584,1024]{2,1,0:T(8,128)(2,1)} %param.12), kind=kOutput, calls=%fused_computation.7 | convolution fusion | flops 7516192768 | bytes 18874368 | tf_op jit(solution)/shard_map/dot_general | solution.py:54
  156.4 12.9 %multiply_convert_fusion = bf16[1024,1024]{1,0:T(8,128)(2,1)S(1)} fusion(f32[1024,1024]{1,0:T(8,128)S(1)} %fusion.4, bf16[1,3584,1024]{2,1,0:T(8,128)(2,1)} %param.11, bf16[128,8,3584]{2,1,0:T(8,128)(2,1)} %all-to-all-done.2), kind=kOutput, calls=%fused_computation.30 | convolution fusion | flops 7522484224 | bytes 20971520 | tf_op jit(solution)/shard_map/dot_general | solution.py:53
  169.3 9.8 %fusion.18 = bf16[128,8,3584]{2,1,0:T(8,128)(2,1)} fusion(bf16[1024,1024]{1,0:T(8,128)(2,1)S(1)} %multiply_convert_fusion, bf16[1,1024,3584]{2,1,0:T(8,128)(2,1)S(1)} %bitcast.73), kind=kOutput, calls=%fused_computation.21 | convolution fusion | flops 7519862784 | bytes 16777216 | tf_op jit(solution)/shard_map/dot_general | solution.py:56
  179.1 1.2 copy-done.1
  180.4 10.2 %all-to-all-start.3 = ((bf16[128,8,3584]{2,1,0:T(8,128)(2,1)}), bf16[128,8,3584]{2,1,0:T(8,128)(2,1)}, u32[]{:S(2)}, u32[]{:S(2)}) async-start(bf16[128,8,3584]{2,1,0:T(8,128)(2,1)} %fusion.18), calls=%async_computation.3 | async-start | bytes 14680064 | tf_op jit(solution)/shard_map/all_to_all | solution.py:91
  190.7 1.6 fusion.43
  192.3 6.8 %gather_fusion = f32[1024]{0:T(1024)S(1)} fusion(f32[128,128]{1,0:T(8,128)S(1)} %fusion.43, s32[1024]{0:T(1024)S(1)} %reshape.134), kind=kCustom, calls=%fused_computation | custom fusion | bytes 16384 | tf_op jit(solution)/shard_map/jit(take_along_axis)/gather | solution.py:69
  199.9 0.8 select_reduce_fusion.1
  200.7 1.8 select_reduce_fusion
  202.5 3.6 %reshape.132 = bf16[256,3584]{1,0:T(8,128)(2,1)S(1)} reshape(bf16[128,56,128]{2,1,0:T(8,128)(2,1)} %copy-done.1) | data formatting | bytes 3670016 | tf_op jit(solution)/shard_map/reshape | solution.py:93
  206.1 1.7 fusion.58
  207.8 70.5 %all-to-all-done.3 = bf16[128,8,3584]{2,1,0:T(8,128)(2,1)} async-done(((bf16[128,8,3584]{2,1,0:T(8,128)(2,1)}), bf16[128,8,3584]{2,1,0:T(8,128)(2,1)}, u32[]{:S(2)}, u32[]{:S(2)}) %all-to-all-start.3) | async-done | bytes 7340064 | tf_op jit(solution)/shard_map/all_to_all | solution.py:91
  278.3 4.2 %fusion = f32[128,3584]{1,0:T(8,128)S(1)} fusion(bf16[128,8,3584]{2,1,0:T(8,128)(2,1)} %all-to-all-done.3, f32[128,1024]{1,0:T(8,128)S(1)} %select_reduce_fusion), kind=kOutput, calls=%fused_computation.3 | convolution fusion | flops 939917312 | bytes 9699328 | tf_op jit(solution)/shard_map/dot_general | solution.py:47
  282.6 4.5 %fusion.25 = f32[128,3584]{1,0:T(8,128)S(1)} fusion(f32[128,3584]{1,0:T(8,128)S(1)} %fusion, bf16[128,8,3584]{2,1,0:T(8,128)(2,1)} %all-to-all-done.3, f32[128,1024]{1,0:T(8,128)S(1)} %select_reduce_fusion), kind=kOutput, calls=%fused_computation.26 | convolution fusion | flops 940244992 | bytes 11534336 | tf_op jit(solution)/shard_map/dot_general | solution.py:47
  287.0 1.5 fusion.28
  (38 shorter events, 1.9 us)
Async XLA Ops:
  0.0 3.2 %copy-start = (bf16[128,3584]{1,0:T(8,128)(2,1)S(1)}, bf16[128,3584]{1,0:T(8,128)(2,1)}, u32[]{:S(2)}) copy-start(bf16[128,3584]{1,0:T(8,128)(2,1)} %param.7) | copy-start | bytes 2752516
  7.1 34.8 %all-to-all-start = ((bf16[128,56,128]{2,1,0:T(8,128)(2,1)}), bf16[128,56,128]{2,1,0:T(8,128)(2,1)S(1)}, u32[]{:S(2)}, u32[]{:S(2)}) async-start(bf16[128,56,128]{2,1,0:T(8,128)(2,1)} %reshape.126), calls=%async_computation | async-start | bytes 3670016 | tf_op jit(solution)/shard_map/all_to_all | solution.py:85
  41.9 96.7 %all-to-all-start.2 = ((bf16[128,8,3584]{2,1,0:T(8,128)(2,1)}), bf16[128,8,3584]{2,1,0:T(8,128)(2,1)}, u32[]{:S(2)}, u32[]{:S(2)}) async-start(bf16[128,8,3584]{2,1,0:T(8,128)(2,1)} %fusion.17), calls=%async_computation.2 | async-start | bytes 14680064 | tf_op jit(solution)/shard_map/all_to_all | solution.py:85
  53.7 6.8 %copy-start.3 = (bf16[256,3584]{1,0:T(8,128)(2,1)S(1)}, bf16[256,3584]{1,0:T(8,128)(2,1)}, u32[]{:S(2)}) copy-start(bf16[256,3584]{1,0:T(8,128)(2,1)} %reshape.128) | copy-start | bytes 5505028
  138.5 40.6 %all-to-all-start.1 = ((bf16[128,56,128]{2,1,0:T(8,128)(2,1)}), bf16[128,56,128]{2,1,0:T(8,128)(2,1)S(1)}, u32[]{:S(2)}, u32[]{:S(2)}) async-start(bf16[128,56,128]{2,1,0:T(8,128)(2,1)} %reshape.129), calls=%async_computation.1 | async-start | bytes 3670016 | tf_op jit(solution)/shard_map/all_to_all | solution.py:91
  145.0 24.3 %slice-start = ((s8[7340032]{0:T(1024)(128)(4,1)}), s8[4194304]{0:T(1024)(128)(4,1)S(1)}, s32[]{:S(2)}) async-start(s8[7340032]{0:T(1024)(128)(4,1)} %bitcast.72), calls=%async_computation.4 | async-start | bytes 8388608
  156.3 12.9 %slice-start.1 = ((s8[7340032]{0:T(1024)(128)(4,1)}), s8[3145728]{0:T(1024)(128)(4,1)S(1)}, s32[]{:S(2)}) async-start(s8[7340032]{0:T(1024)(128)(4,1)} %bitcast.72), calls=%async_computation.5 | async-start | bytes 6291456
  179.1 1.2 copy-start.1
  180.4 97.9 %all-to-all-start.3 = ((bf16[128,8,3584]{2,1,0:T(8,128)(2,1)}), bf16[128,8,3584]{2,1,0:T(8,128)(2,1)}, u32[]{:S(2)}, u32[]{:S(2)}) async-start(bf16[128,8,3584]{2,1,0:T(8,128)(2,1)} %fusion.18), calls=%async_computation.3 | async-start | bytes 14680064 | tf_op jit(solution)/shard_map/all_to_all | solution.py:91
  282.5 4.5 %copy-start.2 = (f32[128,3584]{1,0:T(8,128)S(1)}, f32[128,3584]{1,0:T(8,128)}, u32[]{:S(2)}) copy-start(f32[128,3584]{1,0:T(8,128)} %fusion.58) | copy-start | bytes 5505028

commit v5 on v4

--- a/solution.py
+++ b/solution.py
@@ -44,9 +44,8 @@
     high_part = lax.reduce_precision(dense, exponent_bits=8, mantissa_bits=7)
     high = high_part.astype(jnp.bfloat16)
     low = (dense - high_part).astype(jnp.bfloat16)
-    return jnp.dot(high, rows, preferred_element_type=jnp.float32) + jnp.dot(
-        low, rows, preferred_element_type=jnp.float32
-    )
+    both = jnp.dot(jnp.concatenate([high, low], axis=0), rows, preferred_element_type=jnp.float32)
+    return both[:tok_dev] + both[tok_dev:]
 
 
 def expert_rows(flat_rows, w_gate, w_up, w_down):

time: 289 us -> 284 us (0.983)
    dot_general x4 -> x2, matrix products: 11.8 us -> 9.21 us  [combine_piece(): jnp.dot(jnp.concatenate([high, low], axis=0), rows, preferred_element_typ...]
  transfers between devices with their start and end apart: 4 -> 4, of which waited for: 3 -> 3; matrix products, arithmetic and copies ran while one was open for 29% -> 30% of each run, Pallas kernels for 0% -> 0%
where the time goes in v5:
time: 284 us
  waiting for transfers between devices  149 us (52%)
  matrix products  68.1 us (24%)
  starting transfers between devices  35.8 us (13%)
  local copies, waits for them, and re-layouts  22.3 us (8%)
  other arithmetic  8.52 us (3%)
    all_to_all x2, waiting for transfers between devices, on_device(): lax.all_to_all(send_rows, ('node', 'local'), split_axis=0, concat_axis=0,...  80 us
    all_to_all x2, waiting for transfers between devices, on_device(): lax.all_to_all(produced, ('node', 'local'), split_axis=0, concat_axis=0,...  68.8 us
    dot_general x2, matrix products, expert_rows(): jnp.dot(hidden, w_down[0], preferred_element_type=jnp.float32)  20.6 us
    dot_general x2, matrix products, expert_rows(): jnp.dot(flat_rows, w_gate[0], preferred_element_type=jnp.float32)  19.7 us
    all_to_all x2, starting transfers between devices, on_device(): lax.all_to_all(send_rows, ('node', 'local'), split_axis=0, concat_axis=0,...  19.2 us
    all_to_all x2, starting transfers between devices, on_device(): lax.all_to_all(produced, ('node', 'local'), split_axis=0, concat_axis=0,...  16.6 us
    dot_general x1, matrix products, expert_rows(): up_part = jnp.dot(flat_rows, w_up[0], preferred_element_type=jnp.float32)  11.4 us
    dot_general x2, matrix products, combine_piece(): jnp.dot(jnp.concatenate([high, low], axis=0), rows, preferred_element_typ...  9.21 us
  transfers between devices with their start and end apart: 4, of which 3 were waited for; matrix products, arithmetic and copies ran while one was open for 30% of the time, Pallas kernels for 0%

profile of v5, /device:TPU:14, one launch (start us, length us, event | category | flops | bytes accessed | tf_op | source)
XLA Modules:
  0.0 283.7 jit_solution(11825702143105011920)
XLA Ops:
  0.0 0.8 broadcast_multiply_fusion
  0.8 0.7 bitcast_or_fusion
  1.9 0.2 fusion.50
  2.3 0.4 fusion.48
  2.8 0.4 fusion.40
  3.2 0.6 convolution_convert_fusion.2
  3.8 3.3 %reshape.126 = bf16[128,56,128]{2,1,0:T(8,128)(2,1)} reshape(bf16[256,3584]{1,0:T(8,128)(2,1)S(1)} %convolution_convert_fusion.2) | data formatting | bytes 3670016 | tf_op jit(solution)/shard_map/reshape | solution.py:77
  7.1 10.4 %all-to-all-start = ((bf16[128,56,128]{2,1,0:T(8,128)(2,1)}), bf16[128,56,128]{2,1,0:T(8,128)(2,1)S(1)}, u32[]{:S(2)}, u32[]{:S(2)}) async-start(bf16[128,56,128]{2,1,0:T(8,128)(2,1)} %reshape.126), calls=%async_computation | async-start | bytes 3670016 | tf_op jit(solution)/shard_map/all_to_all | solution.py:84
  17.5 1.9 fusion.22
  19.4 5.0 %fusion.15 = bf16[128,8,3584]{2,1,0:T(8,128)(2,1)} fusion(pred[1024,128]{1,0:T(8,128)(4,1)S(1)} %fusion.22, bf16[128,3584]{1,0:T(8,128)(2,1)S(1)} %copy-done), kind=kOutput, calls=%fused_computation.18 | convolution fusion | flops 943194112 | bytes 8388608 | tf_op jit(solution)/shard_map/dot_general | solution.py:35
  24.4 17.5 %all-to-all-done = bf16[128,56,128]{2,1,0:T(8,128)(2,1)S(1)} async-done(((bf16[128,56,128]{2,1,0:T(8,128)(2,1)}), bf16[128,56,128]{2,1,0:T(8,128)(2,1)S(1)}, u32[]{:S(2)}, u32[]{:S(2)}) %all-to-all-start) | async-done | bytes 1835040 | tf_op jit(solution)/shard_map/all_to_all | solution.py:84
  41.9 8.9 %all-to-all-start.2 = ((bf16[128,8,3584]{2,1,0:T(8,128)(2,1)}), bf16[128,8,3584]{2,1,0:T(8,128)(2,1)}, u32[]{:S(2)}, u32[]{:S(2)}) async-start(bf16[128,8,3584]{2,1,0:T(8,128)(2,1)} %fusion.15), calls=%async_computation.2 | async-start | bytes 14680064 | tf_op jit(solution)/shard_map/all_to_all | solution.py:84
  50.7 3.0 %reshape.128 = bf16[256,3584]{1,0:T(8,128)(2,1)} reshape(bf16[128,56,128]{2,1,0:T(8,128)(2,1)S(1)} %all-to-all-done) | data formatting | bytes 3670016 | tf_op jit(solution)/shard_map/reshape | solution.py:87
  53.7 6.8 %fusion.13 = f32[256,1024]{1,0:T(8,128)} fusion(bf16[256,3584]{1,0:T(8,128)(2,1)} %reshape.128, bf16[1,3584,1024]{2,1,0:T(8,128)(2,1)} %param.11), kind=kOutput, calls=%fused_computation.16 | convolution fusion | flops 1879048192 | bytes 10223616 | tf_op jit(solution)/shard_map/dot_general | solution.py:52
  60.5 10.8 %fusion.19 = bf16[256,3584]{1,0:T(8,128)(2,1)} fusion(bf16[1,1024,3584]{2,1,0:T(8,128)(2,1)} %param.13, bf16[256,3584]{1,0:T(8,128)(2,1)S(1)} %copy-done.2, bf16[1,3584,1024]{2,1,0:T(8,128)(2,1)} %param.12, f32[256,1024]{1,0:T(8,128)} %fusion.13), kind=kOutput, calls=%fused_computation.20 | convolution fusion | flops 3760586752 | bytes 19398656 | tf_op jit(solution)/shard_map/dot_general | solution.py:55
  71.3 4.7 %reshape.129 = bf16[128,56,128]{2,1,0:T(8,128)(2,1)} reshape(bf16[256,3584]{1,0:T(8,128)(2,1)} %fusion.19) | data formatting | bytes 3670016 | tf_op jit(solution)/shard_map/reshape | solution.py:87
  76.0 62.6 %all-to-all-done.2 = bf16[128,8,3584]{2,1,0:T(8,128)(2,1)} async-done(((bf16[128,8,3584]{2,1,0:T(8,128)(2,1)}), bf16[128,8,3584]{2,1,0:T(8,128)(2,1)}, u32[]{:S(2)}, u32[]{:S(2)}) %all-to-all-start.2) | async-done | bytes 7340064 | tf_op jit(solution)/shard_map/all_to_all | solution.py:84
  138.5 6.4 %all-to-all-start.1 = ((bf16[128,56,128]{2,1,0:T(8,128)(2,1)}), bf16[128,56,128]{2,1,0:T(8,128)(2,1)S(1)}, u32[]{:S(2)}, u32[]{:S(2)}) async-start(bf16[128,56,128]{2,1,0:T(8,128)(2,1)} %reshape.129), calls=%async_computation.1 | async-start | bytes 3670016 | tf_op jit(solution)/shard_map/all_to_all | solution.py:90
  145.0 11.4 %fusion.2 = f32[1024,1024]{1,0:T(8,128)S(1)} fusion(bf16[128,8,3584]{2,1,0:T(8,128)(2,1)} %all-to-all-done.2, bf16[1,3584,1024]{2,1,0:T(8,128)(2,1)} %param.12), kind=kOutput, calls=%fused_computation.5 | convolution fusion | flops 7516192768 | bytes 18874368 | tf_op jit(solution)/shard_map/dot_general | solution.py:53
  156.4 12.9 %multiply_convert_fusion = bf16[1024,1024]{1,0:T(8,128)(2,1)S(1)} fusion(f32[1024,1024]{1,0:T(8,128)S(1)} %fusion.2, bf16[1,3584,1024]{2,1,0:T(8,128)(2,1)} %param.11, bf16[128,8,3584]{2,1,0:T(8,128)(2,1)} %all-to-all-done.2), kind=kOutput, calls=%fused_computation.24 | convolution fusion | flops 7522484224 | bytes 20971520 | tf_op jit(solution)/shard_map/dot_general | solution.py:52
  169.3 9.8 %fusion.16 = bf16[128,8,3584]{2,1,0:T(8,128)(2,1)} fusion(bf16[1024,1024]{1,0:T(8,128)(2,1)S(1)} %multiply_convert_fusion, bf16[1,1024,3584]{2,1,0:T(8,128)(2,1)S(1)} %bitcast.68), kind=kOutput, calls=%fused_computation.19 | convolution fusion | flops 7519862784 | bytes 16777216 | tf_op jit(solution)/shard_map/dot_general | solution.py:55
  179.1 10.2 %all-to-all-start.3 = ((bf16[128,8,3584]{2,1,0:T(8,128)(2,1)}), bf16[128,8,3584]{2,1,0:T(8,128)(2,1)}, u32[]{:S(2)}, u32[]{:S(2)}) async-start(bf16[128,8,3584]{2,1,0:T(8,128)(2,1)} %fusion.16), calls=%async_computation.3 | async-start | bytes 14680064 | tf_op jit(solution)/shard_map/all_to_all | solution.py:90
  189.5 1.6 fusion.38
  191.1 6.8 %gather_fusion = f32[1024]{0:T(1024)S(1)} fusion(f32[128,128]{1,0:T(8,128)S(1)} %fusion.38, s32[1024]{0:T(1024)S(1)} %reshape.134), kind=kCustom, calls=%fused_computation | custom fusion | bytes 16384 | tf_op jit(solution)/shard_map/jit(take_along_axis)/gather | solution.py:68
  198.3 0.1 copy.56
  198.6 0.8 select_reduce_fusion.1
  199.5 1.8 select_reduce_fusion
  201.4 3.0 %reshape.132 = bf16[256,3584]{1,0:T(8,128)(2,1)} reshape(bf16[128,56,128]{2,1,0:T(8,128)(2,1)S(1)} %all-to-all-done.1) | data formatting | bytes 3670016 | tf_op jit(solution)/shard_map/reshape | solution.py:92
  204.4 3.9 %fusion.54 = f32[256,3584]{1,0:T(8,128)} fusion(bf16[256,3584]{1,0:T(8,128)(2,1)} %reshape.132, bf16[128,256]{1,0:T(8,128)(2,1)S(1)} %get-tuple-element.24, bf16[128,256]{1,0:T(8,128)(2,1)S(1)} %get-tuple-element.23), kind=kOutput, calls=%fused_computation.62 | convolution fusion | flops 470024192 | bytes 5636096 | tf_op jit(solution)/shard_map/dot_general | solution.py:47
  208.3 68.8 %all-to-all-done.3 = bf16[128,8,3584]{2,1,0:T(8,128)(2,1)} async-done(((bf16[128,8,3584]{2,1,0:T(8,128)(2,1)}), bf16[128,8,3584]{2,1,0:T(8,128)(2,1)}, u32[]{:S(2)}, u32[]{:S(2)}) %all-to-all-start.3) | async-done | bytes 7340064 | tf_op jit(solution)/shard_map/all_to_all | solution.py:90
  277.1 5.3 %fusion = f32[256,3584]{1,0:T(8,128)S(1)} fusion(bf16[128,8,3584]{2,1,0:T(8,128)(2,1)} %all-to-all-done.3, bf16[128,1024]{1,0:T(8,128)(2,1)S(1)} %get-tuple-element.22, bf16[128,1024]{1,0:T(8,128)(2,1)S(1)} %get-tuple-element.21), kind=kOutput, calls=%fused_computation.3 | convolution fusion | flops 1880096768 | bytes 11534336 | tf_op jit(solution)/shard_map/dot_general | solution.py:47
  282.4 1.4 fusion.29
  (37 shorter events, 1.6 us)
Async XLA Ops:
  0.0 3.2 %copy-start = (bf16[128,3584]{1,0:T(8,128)(2,1)S(1)}, bf16[128,3584]{1,0:T(8,128)(2,1)}, u32[]{:S(2)}) copy-start(bf16[128,3584]{1,0:T(8,128)(2,1)} %param.7) | copy-start | bytes 2752516
  7.1 34.8 %all-to-all-start = ((bf16[128,56,128]{2,1,0:T(8,128)(2,1)}), bf16[128,56,128]{2,1,0:T(8,128)(2,1)S(1)}, u32[]{:S(2)}, u32[]{:S(2)}) async-start(bf16[128,56,128]{2,1,0:T(8,128)(2,1)} %reshape.126), calls=%async_computation | async-start | bytes 3670016 | tf_op jit(solution)/shard_map/all_to_all | solution.py:84
  41.9 96.7 %all-to-all-start.2 = ((bf16[128,8,3584]{2,1,0:T(8,128)(2,1)}), bf16[128,8,3584]{2,1,0:T(8,128)(2,1)}, u32[]{:S(2)}, u32[]{:S(2)}) async-start(bf16[128,8,3584]{2,1,0:T(8,128)(2,1)} %fusion.15), calls=%async_computation.2 | async-start | bytes 14680064 | tf_op jit(solution)/shard_map/all_to_all | solution.py:84
  53.7 6.8 %copy-start.2 = (bf16[256,3584]{1,0:T(8,128)(2,1)S(1)}, bf16[256,3584]{1,0:T(8,128)(2,1)}, u32[]{:S(2)}) copy-start(bf16[256,3584]{1,0:T(8,128)(2,1)} %reshape.128) | copy-start | bytes 5505028
  138.5 40.6 %all-to-all-start.1 = ((bf16[128,56,128]{2,1,0:T(8,128)(2,1)}), bf16[128,56,128]{2,1,0:T(8,128)(2,1)S(1)}, u32[]{:S(2)}, u32[]{:S(2)}) async-start(bf16[128,56,128]{2,1,0:T(8,128)(2,1)} %reshape.129), calls=%async_computation.1 | async-start | bytes 3670016 | tf_op jit(solution)/shard_map/all_to_all | solution.py:90
  145.0 24.3 %slice-start = ((s8[7340032]{0:T(1024)(128)(4,1)}), s8[4194304]{0:T(1024)(128)(4,1)S(1)}, s32[]{:S(2)}) async-start(s8[7340032]{0:T(1024)(128)(4,1)} %bitcast.67), calls=%async_computation.4 | async-start | bytes 8388608
  156.3 12.9 %slice-start.1 = ((s8[7340032]{0:T(1024)(128)(4,1)}), s8[3145728]{0:T(1024)(128)(4,1)S(1)}, s32[]{:S(2)}) async-start(s8[7340032]{0:T(1024)(128)(4,1)} %bitcast.67), calls=%async_computation.5 | async-start | bytes 6291456
  179.1 97.9 %all-to-all-start.3 = ((bf16[128,8,3584]{2,1,0:T(8,128)(2,1)}), bf16[128,8,3584]{2,1,0:T(8,128)(2,1)}, u32[]{:S(2)}, u32[]{:S(2)}) async-start(bf16[128,8,3584]{2,1,0:T(8,128)(2,1)} %fusion.16), calls=%async_computation.3 | async-start | bytes 14680064 | tf_op jit(solution)/shard_map/all_to_all | solution.py:90
  277.1 5.3 %copy-start.1 = (f32[256,3584]{1,0:T(8,128)S(1)}, f32[256,3584]{1,0:T(8,128)}, u32[]{:S(2)}) copy-start(f32[256,3584]{1,0:T(8,128)} %fusion.54) | copy-start | bytes 11010052

commit v6 on v5

--- a/solution.py
+++ b/solution.py
@@ -48,9 +48,10 @@
     return both[:tok_dev] + both[tok_dev:]
 
 
-def expert_rows(flat_rows, w_gate, w_up, w_down):
-    gate_part = jnp.dot(flat_rows, w_gate[0], preferred_element_type=jnp.float32)
-    up_part = jnp.dot(flat_rows, w_up[0], preferred_element_type=jnp.float32)
+def expert_rows(flat_rows, w_gate_up, w_down):
+    both = jnp.dot(flat_rows, w_gate_up, preferred_element_type=jnp.float32)
+    ff = w_down.shape[1]
+    gate_part, up_part = both[:, :ff], both[:, ff:]
     hidden = (jax.nn.silu(gate_part) * up_part).astype(jnp.bfloat16)
     return jnp.dot(hidden, w_down[0], preferred_element_type=jnp.float32).astype(jnp.bfloat16)
 
@@ -72,6 +73,7 @@
     pieces = slot_pieces(cap_rows, feat_width)
     weights = 2.5 * picked / picked_total[:, None]
     mixed = jnp.zeros((tok_dev, feat_width), jnp.float32)
+    w_gate_up = jnp.concatenate([w_gate[0], w_up[0]], axis=1)
     starts = [sum(pieces[:i]) for i in range(len(pieces))]
     sent = [
         gather_piece(tokens, flat_ids, positions, start, size, experts_all).reshape(wire_of(size, feat_width, experts_all))
@@ -84,7 +86,7 @@
         received.append(lax.all_to_all(send_rows, ("node", "local"), split_axis=0, concat_axis=0, tiled=True))
     returned = []
     for i, (start, size) in enumerate(zip(starts, pieces)):
-        produced = expert_rows(received[i].reshape(-1, feat_width), w_gate, w_up, w_down).reshape(received[i].shape)
+        produced = expert_rows(received[i].reshape(-1, feat_width), w_gate_up, w_down).reshape(received[i].shape)
         if i:
             returned[-1], produced = lax.optimization_barrier((returned[-1], produced))
         returned.append(lax.all_to_all(produced, ("node", "local"), split_axis=0, concat_axis=0, tiled=True))

time: 284 us -> 288 us (1.014)
  waiting for transfers between devices: 149 us -> 153 us
    all_to_all x2, waiting for transfers between devices: 80 us -> 84.2 us  [on_device(): lax.all_to_all(send_rows, ('node', 'local'), split_axis=0, concat_axis=0,...]
    dot_general x3 -> x2, matrix products: 31.1 us -> 32.4 us  [expert_rows(): both = jnp.dot(flat_rows, w_gate_up, preferred_element_type=jnp.float32)]
where the time goes in v6:
time: 288 us
  waiting for transfers between devices  153 us (53%)
  matrix products  69.6 us (24%)
  starting transfers between devices  35.8 us (12%)
  local copies, waits for them, and re-layouts  20.8 us (7%)
  other arithmetic  8.51 us (3%)
    all_to_all x2, waiting for transfers between devices, on_device(): lax.all_to_all(send_rows, ('node', 'local'), split_axis=0, concat_axis=0,...  84.2 us
    all_to_all x2, waiting for transfers between devices, on_device(): lax.all_to_all(produced, ('node', 'local'), split_axis=0, concat_axis=0,...  68.7 us
    dot_general x2, matrix products, expert_rows(): both = jnp.dot(flat_rows, w_gate_up, preferred_element_type=jnp.float32)  32.4 us
    dot_general x2, matrix products, expert_rows(): jnp.dot(hidden, w_down[0], preferred_element_type=jnp.float32)  20.7 us
    all_to_all x2, starting transfers between devices, on_device(): lax.all_to_all(send_rows, ('node', 'local'), split_axis=0, concat_axis=0,...  19.2 us
    all_to_all x2, starting transfers between devices, on_device(): lax.all_to_all(produced, ('node', 'local'), split_axis=0, concat_axis=0,...  16.6 us
    dot_general x2, matrix products, combine_piece(): jnp.dot(jnp.concatenate([high, low], axis=0), rows, preferred_element_typ...  9.24 us
    gather x5, local copies, waits for them, and re-layouts, on_device(): picked = jnp.take_along_axis(affinity, expert_ids, axis=1)  7.12 us
  transfers between devices with their start and end apart: 4, of which 3 were waited for; matrix products, arithmetic and copies ran while one was open for 30% of the time, Pallas kernels for 0%

profile of v6, /device:TPU:14, one launch (start us, length us, event | category | flops | bytes accessed | tf_op | source)
XLA Modules:
  0.0 287.8 jit_solution(10547993766999074875)
XLA Ops:
  0.0 0.8 broadcast_multiply_fusion
  0.8 0.7 bitcast_or_fusion
  1.9 0.2 fusion.36
  2.3 0.4 fusion.34
  2.8 0.4 fusion.27
  3.2 0.6 convolution_convert_fusion.2
  3.8 3.3 %reshape.126 = bf16[128,56,128]{2,1,0:T(8,128)(2,1)} reshape(bf16[256,3584]{1,0:T(8,128)(2,1)S(1)} %convolution_convert_fusion.2) | data formatting | bytes 3670016 | tf_op jit(solution)/shard_map/reshape | solution.py:79
  7.1 10.4 %all-to-all-start = ((bf16[128,56,128]{2,1,0:T(8,128)(2,1)}), bf16[128,56,128]{2,1,0:T(8,128)(2,1)S(1)}, u32[]{:S(2)}, u32[]{:S(2)}) async-start(bf16[128,56,128]{2,1,0:T(8,128)(2,1)} %reshape.126), calls=%async_computation | async-start | bytes 3670016 | tf_op jit(solution)/shard_map/all_to_all | solution.py:86
  17.5 1.9 fusion.16
  19.4 5.0 %fusion.8 = bf16[128,8,3584]{2,1,0:T(8,128)(2,1)} fusion(pred[1024,128]{1,0:T(8,128)(4,1)S(1)} %fusion.16, bf16[128,3584]{1,0:T(8,128)(2,1)S(1)} %copy-done), kind=kOutput, calls=%fused_computation.12 | convolution fusion | flops 943194112 | bytes 8388608 | tf_op jit(solution)/shard_map/dot_general | solution.py:35
  24.4 17.5 %all-to-all-done = bf16[128,56,128]{2,1,0:T(8,128)(2,1)S(1)} async-done(((bf16[128,56,128]{2,1,0:T(8,128)(2,1)}), bf16[128,56,128]{2,1,0:T(8,128)(2,1)S(1)}, u32[]{:S(2)}, u32[]{:S(2)}) %all-to-all-start) | async-done | bytes 1835040 | tf_op jit(solution)/shard_map/all_to_all | solution.py:86
  41.9 8.9 %all-to-all-start.2 = ((bf16[128,8,3584]{2,1,0:T(8,128)(2,1)}), bf16[128,8,3584]{2,1,0:T(8,128)(2,1)}, u32[]{:S(2)}, u32[]{:S(2)}) async-start(bf16[128,8,3584]{2,1,0:T(8,128)(2,1)} %fusion.8), calls=%async_computation.2 | async-start | bytes 14680064 | tf_op jit(solution)/shard_map/all_to_all | solution.py:86
  50.8 3.0 %reshape.128 = bf16[256,3584]{1,0:T(8,128)(2,1)} reshape(bf16[128,56,128]{2,1,0:T(8,128)(2,1)S(1)} %all-to-all-done) | data formatting | bytes 3670016 | tf_op jit(solution)/shard_map/reshape | solution.py:89
  53.7 9.7 %fusion.1 = f32[256,2048]{1,0:T(8,128)S(1)} fusion(bf16[256,3584]{1,0:T(8,128)(2,1)} %reshape.128, bf16[3584,1024]{1,0:T(8,128)(2,1)} %bitcast.45, bf16[3584,1024]{1,0:T(8,128)(2,1)} %bitcast.47), kind=kOutput, calls=%fused_computation.3 | convolution fusion | flops 3787456512 | bytes 18612224 | tf_op jit(solution)/shard_map/dot_general | solution.py:52
  63.4 5.2 %fusion.12 = bf16[256,3584]{1,0:T(8,128)(2,1)S(1)} fusion(bf16[1,1024,3584]{2,1,0:T(8,128)(2,1)} %param.13, f32[256,2048]{1,0:T(8,128)S(1)} %fusion.1), kind=kOutput, calls=%fused_computation.14 | convolution fusion | flops 1881538560 | bytes 11272192 | tf_op jit(solution)/shard_map/dot_general | solution.py:56
  68.6 3.2 %reshape.129 = bf16[128,56,128]{2,1,0:T(8,128)(2,1)} reshape(bf16[256,3584]{1,0:T(8,128)(2,1)S(1)} %fusion.12) | data formatting | bytes 3670016 | tf_op jit(solution)/shard_map/reshape | solution.py:89
  71.9 66.7 %all-to-all-done.2 = bf16[128,8,3584]{2,1,0:T(8,128)(2,1)} async-done(((bf16[128,8,3584]{2,1,0:T(8,128)(2,1)}), bf16[128,8,3584]{2,1,0:T(8,128)(2,1)}, u32[]{:S(2)}, u32[]{:S(2)}) %all-to-all-start.2) | async-done | bytes 7340064 | tf_op jit(solution)/shard_map/all_to_all | solution.py:86
  138.5 6.4 %all-to-all-start.1 = ((bf16[128,56,128]{2,1,0:T(8,128)(2,1)}), bf16[128,56,128]{2,1,0:T(8,128)(2,1)S(1)}, u32[]{:S(2)}, u32[]{:S(2)}) async-start(bf16[128,56,128]{2,1,0:T(8,128)(2,1)} %reshape.129), calls=%async_computation.1 | async-start | bytes 3670016 | tf_op jit(solution)/shard_map/all_to_all | solution.py:92
  145.0 22.8 %fusion = f32[1024,2048]{1,0:T(8,128)} fusion(bf16[3584,1024]{1,0:T(8,128)(2,1)} %bitcast.46, bf16[3584,1024]{1,0:T(8,128)(2,1)} %bitcast.48, bf16[128,8,3584]{2,1,0:T(8,128)(2,1)} %all-to-all-done.2), kind=kOutput, calls=%fused_computation.2 | convolution fusion | flops 15061745664 | bytes 30408704 | tf_op jit(solution)/shard_map/dot_general | solution.py:52
  167.7 15.4 %fusion.9 = bf16[128,8,3584]{2,1,0:T(8,128)(2,1)} fusion(bf16[1,1024,3584]{2,1,0:T(8,128)(2,1)} %param.13, f32[1024,2048]{1,0:T(8,128)} %fusion), kind=kOutput, calls=%fused_computation.13 | convolution fusion | flops 7526154240 | bytes 23068672 | tf_op jit(solution)/shard_map/dot_general | solution.py:56
  183.2 10.2 %all-to-all-start.3 = ((bf16[128,8,3584]{2,1,0:T(8,128)(2,1)}), bf16[128,8,3584]{2,1,0:T(8,128)(2,1)}, u32[]{:S(2)}, u32[]{:S(2)}) async-start(bf16[128,8,3584]{2,1,0:T(8,128)(2,1)} %fusion.9), calls=%async_computation.3 | async-start | bytes 14680064 | tf_op jit(solution)/shard_map/all_to_all | solution.py:92
  193.5 1.6 fusion.24
  195.1 6.8 %gather_fusion = f32[1024]{0:T(1024)S(1)} fusion(f32[128,128]{1,0:T(8,128)S(1)} %fusion.24, s32[1024]{0:T(1024)S(1)} %reshape.134), kind=kCustom, calls=%fused_computation | custom fusion | bytes 16384 | tf_op jit(solution)/shard_map/jit(take_along_axis)/gather | solution.py:69
  202.3 0.1 copy.56
  202.6 0.1 copy.48
  202.7 0.8 select_reduce_fusion.1
  203.5 1.8 select_reduce_fusion
  205.4 3.0 %reshape.132 = bf16[256,3584]{1,0:T(8,128)(2,1)} reshape(bf16[128,56,128]{2,1,0:T(8,128)(2,1)S(1)} %all-to-all-done.1) | data formatting | bytes 3670016 | tf_op jit(solution)/shard_map/reshape | solution.py:94
  208.4 4.0 %fusion.40 = f32[256,3584]{1,0:T(8,128)} fusion(bf16[256,3584]{1,0:T(8,128)(2,1)} %reshape.132, bf16[128,256]{1,0:T(8,128)(2,1)S(1)} %get-tuple-element.24, bf16[128,256]{1,0:T(8,128)(2,1)S(1)} %get-tuple-element.23), kind=kOutput, calls=%fused_computation.58 | convolution fusion | flops 470024192 | bytes 5636096 | tf_op jit(solution)/shard_map/dot_general | solution.py:47
  212.4 68.7 %all-to-all-done.3 = bf16[128,8,3584]{2,1,0:T(8,128)(2,1)} async-done(((bf16[128,8,3584]{2,1,0:T(8,128)(2,1)}), bf16[128,8,3584]{2,1,0:T(8,128)(2,1)}, u32[]{:S(2)}, u32[]{:S(2)}) %all-to-all-start.3) | async-done | bytes 7340064 | tf_op jit(solution)/shard_map/all_to_all | solution.py:92
  281.1 5.3 %fusion.2 = f32[256,3584]{1,0:T(8,128)S(1)} fusion(bf16[128,8,3584]{2,1,0:T(8,128)(2,1)} %all-to-all-done.3, bf16[128,1024]{1,0:T(8,128)(2,1)S(1)} %get-tuple-element.22, bf16[128,1024]{1,0:T(8,128)(2,1)S(1)} %get-tuple-element.21), kind=kOutput, calls=%fused_computation.6 | convolution fusion | flops 1880096768 | bytes 11534336 | tf_op jit(solution)/shard_map/dot_general | solution.py:47
  286.4 1.4 fusion.21
  (29 shorter events, 1.5 us)
Async XLA Ops:
  0.0 3.2 %copy-start = (bf16[128,3584]{1,0:T(8,128)(2,1)S(1)}, bf16[128,3584]{1,0:T(8,128)(2,1)}, u32[]{:S(2)}) copy-start(bf16[128,3584]{1,0:T(8,128)(2,1)} %param.7) | copy-start | bytes 2752516
  7.1 34.8 %all-to-all-start = ((bf16[128,56,128]{2,1,0:T(8,128)(2,1)}), bf16[128,56,128]{2,1,0:T(8,128)(2,1)S(1)}, u32[]{:S(2)}, u32[]{:S(2)}) async-start(bf16[128,56,128]{2,1,0:T(8,128)(2,1)} %reshape.126), calls=%async_computation | async-start | bytes 3670016 | tf_op jit(solution)/shard_map/all_to_all | solution.py:86
  41.9 96.7 %all-to-all-start.2 = ((bf16[128,8,3584]{2,1,0:T(8,128)(2,1)}), bf16[128,8,3584]{2,1,0:T(8,128)(2,1)}, u32[]{:S(2)}, u32[]{:S(2)}) async-start(bf16[128,8,3584]{2,1,0:T(8,128)(2,1)} %fusion.8), calls=%async_computation.2 | async-start | bytes 14680064 | tf_op jit(solution)/shard_map/all_to_all | solution.py:86
  138.5 44.6 %all-to-all-start.1 = ((bf16[128,56,128]{2,1,0:T(8,128)(2,1)}), bf16[128,56,128]{2,1,0:T(8,128)(2,1)S(1)}, u32[]{:S(2)}, u32[]{:S(2)}) async-start(bf16[128,56,128]{2,1,0:T(8,128)(2,1)} %reshape.129), calls=%async_computation.1 | async-start | bytes 3670016 | tf_op jit(solution)/shard_map/all_to_all | solution.py:92
  183.2 97.9 %all-to-all-start.3 = ((bf16[128,8,3584]{2,1,0:T(8,128)(2,1)}), bf16[128,8,3584]{2,1,0:T(8,128)(2,1)}, u32[]{:S(2)}, u32[]{:S(2)}) async-start(bf16[128,8,3584]{2,1,0:T(8,128)(2,1)} %fusion.9), calls=%async_computation.3 | async-start | bytes 14680064 | tf_op jit(solution)/shard_map/all_to_all | solution.py:92
  281.1 5.3 %copy-start.1 = (f32[256,3584]{1,0:T(8,128)S(1)}, f32[256,3584]{1,0:T(8,128)}, u32[]{:S(2)}) copy-start(f32[256,3584]{1,0:T(8,128)} %fusion.40) | copy-start | bytes 11010052

commit v7 on v5

--- a/solution.py
+++ b/solution.py
@@ -44,8 +44,8 @@
     high_part = lax.reduce_precision(dense, exponent_bits=8, mantissa_bits=7)
     high = high_part.astype(jnp.bfloat16)
     low = (dense - high_part).astype(jnp.bfloat16)
-    both = jnp.dot(jnp.concatenate([high, low], axis=0), rows, preferred_element_type=jnp.float32)
-    return both[:tok_dev] + both[tok_dev:]
+    stacked = jnp.concatenate([high, low], axis=1)
+    return jnp.dot(stacked, jnp.concatenate([rows, rows], axis=0), preferred_element_type=jnp.float32)
 
 
 def expert_rows(flat_rows, w_gate, w_up, w_down):

time: 284 us -> 286 us (level)
  waiting for transfers between devices: 149 us -> 153 us
    all_to_all x2, waiting for transfers between devices: 68.8 us -> 72.7 us  [on_device(): lax.all_to_all(produced, ('node', 'local'), split_axis=0, concat_axis=0,...]
  transfers between devices with their start and end apart: 4 -> 4, of which waited for: 3 -> 3; matrix products, arithmetic and copies ran while one was open for 30% -> 28% of each run, Pallas kernels for 0% -> 0%
where the time goes in v7:
time: 286 us; the launch traced here: 285 us
  waiting for transfers between devices  153 us (53%)
  matrix products  67 us (23%)
  starting transfers between devices  35.8 us (13%)
  local copies, waits for them, and re-layouts  22.2 us (8%)
  other arithmetic  7.16 us (3%)
    all_to_all x2, waiting for transfers between devices, on_device(): lax.all_to_all(send_rows, ('node', 'local'), split_axis=0, concat_axis=0,...  80 us
    all_to_all x2, waiting for transfers between devices, on_device(): lax.all_to_all(produced, ('node', 'local'), split_axis=0, concat_axis=0,...  72.7 us
    dot_general x2, matrix products, expert_rows(): jnp.dot(hidden, w_down[0], preferred_element_type=jnp.float32)  20.6 us
    dot_general x2, matrix products, expert_rows(): jnp.dot(flat_rows, w_gate[0], preferred_element_type=jnp.float32)  19.7 us
    all_to_all x2, starting transfers between devices, on_device(): lax.all_to_all(send_rows, ('node', 'local'), split_axis=0, concat_axis=0,...  19.2 us
    all_to_all x2, starting transfers between devices, on_device(): lax.all_to_all(produced, ('node', 'local'), split_axis=0, concat_axis=0,...  16.6 us
    dot_general x1, matrix products, expert_rows(): up_part = jnp.dot(flat_rows, w_up[0], preferred_element_type=jnp.float32)  11.4 us
    dot_general x2, matrix products, combine_piece(): jnp.dot(stacked, jnp.concatenate([rows, rows], axis=0), preferred_element...  8.1 us
  transfers between devices with their start and end apart: 4, of which 3 were waited for; matrix products, arithmetic and copies ran while one was open for 28% of the time, Pallas kernels for 0%

profile of v7, /device:TPU:14, one launch (start us, length us, event | category | flops | bytes accessed | tf_op | source)
XLA Modules:
  0.0 285.2 jit_solution(16376236350480248526)
XLA Ops:
  0.0 0.8 broadcast_multiply_fusion
  0.8 0.7 bitcast_or_fusion
  1.9 0.2 fusion.54
  2.3 0.4 fusion.52
  2.8 0.4 fusion.44
  3.2 0.6 convolution_convert_fusion.2
  3.8 3.3 %reshape.126 = bf16[128,56,128]{2,1,0:T(8,128)(2,1)} reshape(bf16[256,3584]{1,0:T(8,128)(2,1)S(1)} %convolution_convert_fusion.2) | data formatting | bytes 3670016 | tf_op jit(solution)/shard_map/reshape | solution.py:77
  7.1 10.4 %all-to-all-start = ((bf16[128,56,128]{2,1,0:T(8,128)(2,1)}), bf16[128,56,128]{2,1,0:T(8,128)(2,1)S(1)}, u32[]{:S(2)}, u32[]{:S(2)}) async-start(bf16[128,56,128]{2,1,0:T(8,128)(2,1)} %reshape.126), calls=%async_computation | async-start | bytes 3670016 | tf_op jit(solution)/shard_map/all_to_all | solution.py:84
  17.5 1.9 fusion.25
  19.4 5.0 %fusion.17 = bf16[128,8,3584]{2,1,0:T(8,128)(2,1)} fusion(pred[1024,128]{1,0:T(8,128)(4,1)S(1)} %fusion.25, bf16[128,3584]{1,0:T(8,128)(2,1)S(1)} %copy-done), kind=kOutput, calls=%fused_computation.20 | convolution fusion | flops 943194112 | bytes 8388608 | tf_op jit(solution)/shard_map/dot_general | solution.py:35
  24.4 17.5 %all-to-all-done = bf16[128,56,128]{2,1,0:T(8,128)(2,1)S(1)} async-done(((bf16[128,56,128]{2,1,0:T(8,128)(2,1)}), bf16[128,56,128]{2,1,0:T(8,128)(2,1)S(1)}, u32[]{:S(2)}, u32[]{:S(2)}) %all-to-all-start) | async-done | bytes 1835040 | tf_op jit(solution)/shard_map/all_to_all | solution.py:84
  41.9 8.9 %all-to-all-start.2 = ((bf16[128,8,3584]{2,1,0:T(8,128)(2,1)}), bf16[128,8,3584]{2,1,0:T(8,128)(2,1)}, u32[]{:S(2)}, u32[]{:S(2)}) async-start(bf16[128,8,3584]{2,1,0:T(8,128)(2,1)} %fusion.17), calls=%async_computation.2 | async-start | bytes 14680064 | tf_op jit(solution)/shard_map/all_to_all | solution.py:84
  50.7 3.0 %reshape.128 = bf16[256,3584]{1,0:T(8,128)(2,1)} reshape(bf16[128,56,128]{2,1,0:T(8,128)(2,1)S(1)} %all-to-all-done) | data formatting | bytes 3670016 | tf_op jit(solution)/shard_map/reshape | solution.py:87
  53.7 6.8 %fusion.15 = f32[256,1024]{1,0:T(8,128)} fusion(bf16[256,3584]{1,0:T(8,128)(2,1)} %reshape.128, bf16[1,3584,1024]{2,1,0:T(8,128)(2,1)} %param.11), kind=kOutput, calls=%fused_computation.18 | convolution fusion | flops 1879048192 | bytes 10223616 | tf_op jit(solution)/shard_map/dot_general | solution.py:52
  60.5 10.8 %fusion.21 = bf16[256,3584]{1,0:T(8,128)(2,1)} fusion(bf16[1,1024,3584]{2,1,0:T(8,128)(2,1)} %param.13, bf16[256,3584]{1,0:T(8,128)(2,1)S(1)} %copy-done.2, bf16[1,3584,1024]{2,1,0:T(8,128)(2,1)} %param.12, f32[256,1024]{1,0:T(8,128)} %fusion.15), kind=kOutput, calls=%fused_computation.22 | convolution fusion | flops 3760586752 | bytes 19398656 | tf_op jit(solution)/shard_map/dot_general | solution.py:55
  71.3 4.7 %reshape.129 = bf16[128,56,128]{2,1,0:T(8,128)(2,1)} reshape(bf16[256,3584]{1,0:T(8,128)(2,1)} %fusion.21) | data formatting | bytes 3670016 | tf_op jit(solution)/shard_map/reshape | solution.py:87
  76.0 62.6 %all-to-all-done.2 = bf16[128,8,3584]{2,1,0:T(8,128)(2,1)} async-done(((bf16[128,8,3584]{2,1,0:T(8,128)(2,1)}), bf16[128,8,3584]{2,1,0:T(8,128)(2,1)}, u32[]{:S(2)}, u32[]{:S(2)}) %all-to-all-start.2) | async-done | bytes 7340064 | tf_op jit(solution)/shard_map/all_to_all | solution.py:84
  138.5 6.4 %all-to-all-start.1 = ((bf16[128,56,128]{2,1,0:T(8,128)(2,1)}), bf16[128,56,128]{2,1,0:T(8,128)(2,1)S(1)}, u32[]{:S(2)}, u32[]{:S(2)}) async-start(bf16[128,56,128]{2,1,0:T(8,128)(2,1)} %reshape.129), calls=%async_computation.1 | async-start | bytes 3670016 | tf_op jit(solution)/shard_map/all_to_all | solution.py:90
  145.0 11.4 %fusion.4 = f32[1024,1024]{1,0:T(8,128)S(1)} fusion(bf16[128,8,3584]{2,1,0:T(8,128)(2,1)} %all-to-all-done.2, bf16[1,3584,1024]{2,1,0:T(8,128)(2,1)} %param.12), kind=kOutput, calls=%fused_computation.7 | convolution fusion | flops 7516192768 | bytes 18874368 | tf_op jit(solution)/shard_map/dot_general | solution.py:53
  156.4 12.9 %multiply_convert_fusion = bf16[1024,1024]{1,0:T(8,128)(2,1)S(1)} fusion(f32[1024,1024]{1,0:T(8,128)S(1)} %fusion.4, bf16[1,3584,1024]{2,1,0:T(8,128)(2,1)} %param.11, bf16[128,8,3584]{2,1,0:T(8,128)(2,1)} %all-to-all-done.2), kind=kOutput, calls=%fused_computation.28 | convolution fusion | flops 7522484224 | bytes 20971520 | tf_op jit(solution)/shard_map/dot_general | solution.py:52
  169.3 9.8 %fusion.18 = bf16[128,8,3584]{2,1,0:T(8,128)(2,1)} fusion(bf16[1024,1024]{1,0:T(8,128)(2,1)S(1)} %multiply_convert_fusion, bf16[1,1024,3584]{2,1,0:T(8,128)(2,1)S(1)} %bitcast.65), kind=kOutput, calls=%fused_computation.21 | convolution fusion | flops 7519862784 | bytes 16777216 | tf_op jit(solution)/shard_map/dot_general | solution.py:55
  179.1 10.2 %all-to-all-start.3 = ((bf16[128,8,3584]{2,1,0:T(8,128)(2,1)}), bf16[128,8,3584]{2,1,0:T(8,128)(2,1)}, u32[]{:S(2)}, u32[]{:S(2)}) async-start(bf16[128,8,3584]{2,1,0:T(8,128)(2,1)} %fusion.18), calls=%async_computation.3 | async-start | bytes 14680064 | tf_op jit(solution)/shard_map/all_to_all | solution.py:90
  189.4 0.1 copy.56
  189.7 1.6 fusion.42
  191.3 6.8 %gather_fusion = f32[1024]{0:T(1024)S(1)} fusion(f32[128,128]{1,0:T(8,128)S(1)} %fusion.42, s32[1024]{0:T(1024)S(1)} %reshape.134), kind=kCustom, calls=%fused_computation | custom fusion | bytes 16384 | tf_op jit(solution)/shard_map/jit(take_along_axis)/gather | solution.py:68
  198.5 0.1 copy.48
  198.6 0.8 select_reduce_fusion.1
  199.5 1.8 select_reduce_fusion
  201.4 3.0 %reshape.132 = bf16[256,3584]{1,0:T(8,128)(2,1)} reshape(bf16[128,56,128]{2,1,0:T(8,128)(2,1)S(1)} %all-to-all-done.1) | data formatting | bytes 3670016 | tf_op jit(solution)/shard_map/reshape | solution.py:92
  204.4 72.7 %all-to-all-done.3 = bf16[128,8,3584]{2,1,0:T(8,128)(2,1)} async-done(((bf16[128,8,3584]{2,1,0:T(8,128)(2,1)}), bf16[128,8,3584]{2,1,0:T(8,128)(2,1)}, u32[]{:S(2)}, u32[]{:S(2)}) %all-to-all-start.3) | async-done | bytes 7340064 | tf_op jit(solution)/shard_map/all_to_all | solution.py:90
  277.1 6.5 %fusion = f32[128,3584]{1,0:T(8,128)S(1)} fusion(bf16[1024,3584]{1,0:T(8,128)(2,1)} %bitcast.11, bf16[128,1024]{1,0:T(8,128)(2,1)S(1)} %get-tuple-element.22, bf16[128,1024]{1,0:T(8,128)(2,1)S(1)} %get-tuple-element.21), kind=kOutput, calls=%fused_computation.1 | convolution fusion | flops 1909456896 | bytes 9699328 | tf_op jit(solution)/shard_map/dot_general | solution.py:48
  283.6 1.6 fusion.24
  (36 shorter events, 1.5 us)
Async XLA Ops:
  0.0 3.2 %copy-start = (bf16[128,3584]{1,0:T(8,128)(2,1)S(1)}, bf16[128,3584]{1,0:T(8,128)(2,1)}, u32[]{:S(2)}) copy-start(bf16[128,3584]{1,0:T(8,128)(2,1)} %param.7) | copy-start | bytes 2752516
  7.1 34.8 %all-to-all-start = ((bf16[128,56,128]{2,1,0:T(8,128)(2,1)}), bf16[128,56,128]{2,1,0:T(8,128)(2,1)S(1)}, u32[]{:S(2)}, u32[]{:S(2)}) async-start(bf16[128,56,128]{2,1,0:T(8,128)(2,1)} %reshape.126), calls=%async_computation | async-start | bytes 3670016 | tf_op jit(solution)/shard_map/all_to_all | solution.py:84
  41.9 96.7 %all-to-all-start.2 = ((bf16[128,8,3584]{2,1,0:T(8,128)(2,1)}), bf16[128,8,3584]{2,1,0:T(8,128)(2,1)}, u32[]{:S(2)}, u32[]{:S(2)}) async-start(bf16[128,8,3584]{2,1,0:T(8,128)(2,1)} %fusion.17), calls=%async_computation.2 | async-start | bytes 14680064 | tf_op jit(solution)/shard_map/all_to_all | solution.py:84
  53.7 6.8 %copy-start.2 = (bf16[256,3584]{1,0:T(8,128)(2,1)S(1)}, bf16[256,3584]{1,0:T(8,128)(2,1)}, u32[]{:S(2)}) copy-start(bf16[256,3584]{1,0:T(8,128)(2,1)} %reshape.128) | copy-start | bytes 5505028
  138.5 40.6 %all-to-all-start.1 = ((bf16[128,56,128]{2,1,0:T(8,128)(2,1)}), bf16[128,56,128]{2,1,0:T(8,128)(2,1)S(1)}, u32[]{:S(2)}, u32[]{:S(2)}) async-start(bf16[128,56,128]{2,1,0:T(8,128)(2,1)} %reshape.129), calls=%async_computation.1 | async-start | bytes 3670016 | tf_op jit(solution)/shard_map/all_to_all | solution.py:90
  145.0 24.3 %slice-start = ((s8[7340032]{0:T(1024)(128)(4,1)}), s8[4194304]{0:T(1024)(128)(4,1)S(1)}, s32[]{:S(2)}) async-start(s8[7340032]{0:T(1024)(128)(4,1)} %bitcast.64), calls=%async_computation.4 | async-start | bytes 8388608
  156.3 12.9 %slice-start.1 = ((s8[7340032]{0:T(1024)(128)(4,1)}), s8[3145728]{0:T(1024)(128)(4,1)S(1)}, s32[]{:S(2)}) async-start(s8[7340032]{0:T(1024)(128)(4,1)} %bitcast.64), calls=%async_computation.5 | async-start | bytes 6291456
  179.1 97.9 %all-to-all-start.3 = ((bf16[128,8,3584]{2,1,0:T(8,128)(2,1)}), bf16[128,8,3584]{2,1,0:T(8,128)(2,1)}, u32[]{:S(2)}, u32[]{:S(2)}) async-start(bf16[128,8,3584]{2,1,0:T(8,128)(2,1)} %fusion.18), calls=%async_computation.3 | async-start | bytes 14680064 | tf_op jit(solution)/shard_map/all_to_all | solution.py:90
  277.1 6.5 %copy-start.1 = (bf16[256,3584]{1,0:T(8,128)(2,1)S(1)}, bf16[256,3584]{1,0:T(8,128)(2,1)}, u32[]{:S(2)}) copy-start(bf16[256,3584]{1,0:T(8,128)(2,1)} %reshape.132) | copy-start | bytes 5505028

commit v8 on v5

--- a/solution.py
+++ b/solution.py
@@ -85,8 +85,6 @@
     returned = []
     for i, (start, size) in enumerate(zip(starts, pieces)):
         produced = expert_rows(received[i].reshape(-1, feat_width), w_gate, w_up, w_down).reshape(received[i].shape)
-        if i:
-            returned[-1], produced = lax.optimization_barrier((returned[-1], produced))
         returned.append(lax.all_to_all(produced, ("node", "local"), split_axis=0, concat_axis=0, tiled=True))
     for i, (start, size) in enumerate(zip(starts, pieces)):
         rows = returned[i].reshape(-1, feat_width)

time: 284 us -> 284 us (level)
  no operation moved by 1% of the time
where the time goes in v8:
time: 284 us
  waiting for transfers between devices  149 us (52%)
  matrix products  68.1 us (24%)
  starting transfers between devices  35.8 us (13%)
  local copies, waits for them, and re-layouts  22.3 us (8%)
  other arithmetic  8.52 us (3%)
    all_to_all x2, waiting for transfers between devices, on_device(): lax.all_to_all(send_rows, ('node', 'local'), split_axis=0, concat_axis=0,...  80 us
    all_to_all x2, waiting for transfers between devices, on_device(): lax.all_to_all(produced, ('node', 'local'), split_axis=0, concat_axis=0,...  68.8 us
    dot_general x2, matrix products, expert_rows(): jnp.dot(hidden, w_down[0], preferred_element_type=jnp.float32)  20.6 us
    dot_general x2, matrix products, expert_rows(): jnp.dot(flat_rows, w_gate[0], preferred_element_type=jnp.float32)  19.7 us
    all_to_all x2, starting transfers between devices, on_device(): lax.all_to_all(send_rows, ('node', 'local'), split_axis=0, concat_axis=0,...  19.2 us
    all_to_all x2, starting transfers between devices, on_device(): lax.all_to_all(produced, ('node', 'local'), split_axis=0, concat_axis=0,...  16.6 us
    dot_general x1, matrix products, expert_rows(): up_part = jnp.dot(flat_rows, w_up[0], preferred_element_type=jnp.float32)  11.4 us
    dot_general x2, matrix products, combine_piece(): jnp.dot(jnp.concatenate([high, low], axis=0), rows, preferred_element_typ...  9.21 us
  transfers between devices with their start and end apart: 4, of which 3 were waited for; matrix products, arithmetic and copies ran while one was open for 30% of the time, Pallas kernels for 0%

profile of v8, /device:TPU:14, one launch (start us, length us, event | category | flops | bytes accessed | tf_op | source)
XLA Modules:
  0.0 283.7 jit_solution(11825702143105011920)
XLA Ops:
  0.0 0.8 broadcast_multiply_fusion
  0.8 0.7 bitcast_or_fusion
  1.9 0.2 fusion.50
  2.3 0.4 fusion.48
  2.8 0.4 fusion.40
  3.2 0.6 convolution_convert_fusion.2
  3.8 3.3 %reshape.126 = bf16[128,56,128]{2,1,0:T(8,128)(2,1)} reshape(bf16[256,3584]{1,0:T(8,128)(2,1)S(1)} %convolution_convert_fusion.2) | data formatting | bytes 3670016 | tf_op jit(solution)/shard_map/reshape | solution.py:77
  7.1 10.4 %all-to-all-start = ((bf16[128,56,128]{2,1,0:T(8,128)(2,1)}), bf16[128,56,128]{2,1,0:T(8,128)(2,1)S(1)}, u32[]{:S(2)}, u32[]{:S(2)}) async-start(bf16[128,56,128]{2,1,0:T(8,128)(2,1)} %reshape.126), calls=%async_computation | async-start | bytes 3670016 | tf_op jit(solution)/shard_map/all_to_all | solution.py:84
  17.5 1.9 fusion.22
  19.4 5.0 %fusion.15 = bf16[128,8,3584]{2,1,0:T(8,128)(2,1)} fusion(pred[1024,128]{1,0:T(8,128)(4,1)S(1)} %fusion.22, bf16[128,3584]{1,0:T(8,128)(2,1)S(1)} %copy-done), kind=kOutput, calls=%fused_computation.18 | convolution fusion | flops 943194112 | bytes 8388608 | tf_op jit(solution)/shard_map/dot_general | solution.py:35
  24.4 17.5 %all-to-all-done = bf16[128,56,128]{2,1,0:T(8,128)(2,1)S(1)} async-done(((bf16[128,56,128]{2,1,0:T(8,128)(2,1)}), bf16[128,56,128]{2,1,0:T(8,128)(2,1)S(1)}, u32[]{:S(2)}, u32[]{:S(2)}) %all-to-all-start) | async-done | bytes 1835040 | tf_op jit(solution)/shard_map/all_to_all | solution.py:84
  41.9 8.9 %all-to-all-start.2 = ((bf16[128,8,3584]{2,1,0:T(8,128)(2,1)}), bf16[128,8,3584]{2,1,0:T(8,128)(2,1)}, u32[]{:S(2)}, u32[]{:S(2)}) async-start(bf16[128,8,3584]{2,1,0:T(8,128)(2,1)} %fusion.15), calls=%async_computation.2 | async-start | bytes 14680064 | tf_op jit(solution)/shard_map/all_to_all | solution.py:84
  50.7 3.0 %reshape.128 = bf16[256,3584]{1,0:T(8,128)(2,1)} reshape(bf16[128,56,128]{2,1,0:T(8,128)(2,1)S(1)} %all-to-all-done) | data formatting | bytes 3670016 | tf_op jit(solution)/shard_map/reshape | solution.py:87
  53.7 6.8 %fusion.13 = f32[256,1024]{1,0:T(8,128)} fusion(bf16[256,3584]{1,0:T(8,128)(2,1)} %reshape.128, bf16[1,3584,1024]{2,1,0:T(8,128)(2,1)} %param.11), kind=kOutput, calls=%fused_computation.16 | convolution fusion | flops 1879048192 | bytes 10223616 | tf_op jit(solution)/shard_map/dot_general | solution.py:52
  60.5 10.8 %fusion.19 = bf16[256,3584]{1,0:T(8,128)(2,1)} fusion(bf16[1,1024,3584]{2,1,0:T(8,128)(2,1)} %param.13, bf16[256,3584]{1,0:T(8,128)(2,1)S(1)} %copy-done.2, bf16[1,3584,1024]{2,1,0:T(8,128)(2,1)} %param.12, f32[256,1024]{1,0:T(8,128)} %fusion.13), kind=kOutput, calls=%fused_computation.20 | convolution fusion | flops 3760586752 | bytes 19398656 | tf_op jit(solution)/shard_map/dot_general | solution.py:55
  71.3 4.7 %reshape.129 = bf16[128,56,128]{2,1,0:T(8,128)(2,1)} reshape(bf16[256,3584]{1,0:T(8,128)(2,1)} %fusion.19) | data formatting | bytes 3670016 | tf_op jit(solution)/shard_map/reshape | solution.py:87
  76.0 62.6 %all-to-all-done.2 = bf16[128,8,3584]{2,1,0:T(8,128)(2,1)} async-done(((bf16[128,8,3584]{2,1,0:T(8,128)(2,1)}), bf16[128,8,3584]{2,1,0:T(8,128)(2,1)}, u32[]{:S(2)}, u32[]{:S(2)}) %all-to-all-start.2) | async-done | bytes 7340064 | tf_op jit(solution)/shard_map/all_to_all | solution.py:84
  138.5 6.4 %all-to-all-start.1 = ((bf16[128,56,128]{2,1,0:T(8,128)(2,1)}), bf16[128,56,128]{2,1,0:T(8,128)(2,1)S(1)}, u32[]{:S(2)}, u32[]{:S(2)}) async-start(bf16[128,56,128]{2,1,0:T(8,128)(2,1)} %reshape.129), calls=%async_computation.1 | async-start | bytes 3670016 | tf_op jit(solution)/shard_map/all_to_all | solution.py:88
  145.0 11.4 %fusion.2 = f32[1024,1024]{1,0:T(8,128)S(1)} fusion(bf16[128,8,3584]{2,1,0:T(8,128)(2,1)} %all-to-all-done.2, bf16[1,3584,1024]{2,1,0:T(8,128)(2,1)} %param.12), kind=kOutput, calls=%fused_computation.5 | convolution fusion | flops 7516192768 | bytes 18874368 | tf_op jit(solution)/shard_map/dot_general | solution.py:53
  156.4 12.9 %multiply_convert_fusion = bf16[1024,1024]{1,0:T(8,128)(2,1)S(1)} fusion(f32[1024,1024]{1,0:T(8,128)S(1)} %fusion.2, bf16[1,3584,1024]{2,1,0:T(8,128)(2,1)} %param.11, bf16[128,8,3584]{2,1,0:T(8,128)(2,1)} %all-to-all-done.2), kind=kOutput, calls=%fused_computation.22 | convolution fusion | flops 7522484224 | bytes 20971520 | tf_op jit(solution)/shard_map/dot_general | solution.py:52
  169.3 9.8 %fusion.16 = bf16[128,8,3584]{2,1,0:T(8,128)(2,1)} fusion(bf16[1024,1024]{1,0:T(8,128)(2,1)S(1)} %multiply_convert_fusion, bf16[1,1024,3584]{2,1,0:T(8,128)(2,1)S(1)} %bitcast.68), kind=kOutput, calls=%fused_computation.19 | convolution fusion | flops 7519862784 | bytes 16777216 | tf_op jit(solution)/shard_map/dot_general | solution.py:55
  179.1 10.2 %all-to-all-start.3 = ((bf16[128,8,3584]{2,1,0:T(8,128)(2,1)}), bf16[128,8,3584]{2,1,0:T(8,128)(2,1)}, u32[]{:S(2)}, u32[]{:S(2)}) async-start(bf16[128,8,3584]{2,1,0:T(8,128)(2,1)} %fusion.16), calls=%async_computation.3 | async-start | bytes 14680064 | tf_op jit(solution)/shard_map/all_to_all | solution.py:88
  189.5 1.6 fusion.38
  191.1 6.8 %gather_fusion = f32[1024]{0:T(1024)S(1)} fusion(f32[128,128]{1,0:T(8,128)S(1)} %fusion.38, s32[1024]{0:T(1024)S(1)} %reshape.134), kind=kCustom, calls=%fused_computation | custom fusion | bytes 16384 | tf_op jit(solution)/shard_map/jit(take_along_axis)/gather | solution.py:68
  198.3 0.1 copy.56
  198.6 0.8 select_reduce_fusion.1
  199.5 1.8 select_reduce_fusion
  201.4 3.0 %reshape.130 = bf16[256,3584]{1,0:T(8,128)(2,1)} reshape(bf16[128,56,128]{2,1,0:T(8,128)(2,1)S(1)} %all-to-all-done.1) | data formatting | bytes 3670016 | tf_op jit(solution)/shard_map/reshape | solution.py:90
  204.4 3.9 %fusion.54 = f32[256,3584]{1,0:T(8,128)} fusion(bf16[256,3584]{1,0:T(8,128)(2,1)} %reshape.130, bf16[128,256]{1,0:T(8,128)(2,1)S(1)} %get-tuple-element.20, bf16[128,256]{1,0:T(8,128)(2,1)S(1)} %get-tuple-element.19), kind=kOutput, calls=%fused_computation.62 | convolution fusion | flops 470024192 | bytes 5636096 | tf_op jit(solution)/shard_map/dot_general | solution.py:47
  208.3 68.8 %all-to-all-done.3 = bf16[128,8,3584]{2,1,0:T(8,128)(2,1)} async-done(((bf16[128,8,3584]{2,1,0:T(8,128)(2,1)}), bf16[128,8,3584]{2,1,0:T(8,128)(2,1)}, u32[]{:S(2)}, u32[]{:S(2)}) %all-to-all-start.3) | async-done | bytes 7340064 | tf_op jit(solution)/shard_map/all_to_all | solution.py:88
  277.1 5.3 %fusion = f32[256,3584]{1,0:T(8,128)S(1)} fusion(bf16[128,8,3584]{2,1,0:T(8,128)(2,1)} %all-to-all-done.3, bf16[128,1024]{1,0:T(8,128)(2,1)S(1)} %get-tuple-element.18, bf16[128,1024]{1,0:T(8,128)(2,1)S(1)} %get-tuple-element.17), kind=kOutput, calls=%fused_computation.3 | convolution fusion | flops 1880096768 | bytes 11534336 | tf_op jit(solution)/shard_map/dot_general | solution.py:47
  282.4 1.4 fusion.29
  (37 shorter events, 1.6 us)
Async XLA Ops:
  0.0 3.2 %copy-start = (bf16[128,3584]{1,0:T(8,128)(2,1)S(1)}, bf16[128,3584]{1,0:T(8,128)(2,1)}, u32[]{:S(2)}) copy-start(bf16[128,3584]{1,0:T(8,128)(2,1)} %param.7) | copy-start | bytes 2752516
  7.1 34.8 %all-to-all-start = ((bf16[128,56,128]{2,1,0:T(8,128)(2,1)}), bf16[128,56,128]{2,1,0:T(8,128)(2,1)S(1)}, u32[]{:S(2)}, u32[]{:S(2)}) async-start(bf16[128,56,128]{2,1,0:T(8,128)(2,1)} %reshape.126), calls=%async_computation | async-start | bytes 3670016 | tf_op jit(solution)/shard_map/all_to_all | solution.py:84
  41.9 96.7 %all-to-all-start.2 = ((bf16[128,8,3584]{2,1,0:T(8,128)(2,1)}), bf16[128,8,3584]{2,1,0:T(8,128)(2,1)}, u32[]{:S(2)}, u32[]{:S(2)}) async-start(bf16[128,8,3584]{2,1,0:T(8,128)(2,1)} %fusion.15), calls=%async_computation.2 | async-start | bytes 14680064 | tf_op jit(solution)/shard_map/all_to_all | solution.py:84
  53.7 6.8 %copy-start.2 = (bf16[256,3584]{1,0:T(8,128)(2,1)S(1)}, bf16[256,3584]{1,0:T(8,128)(2,1)}, u32[]{:S(2)}) copy-start(bf16[256,3584]{1,0:T(8,128)(2,1)} %reshape.128) | copy-start | bytes 5505028
  138.5 40.6 %all-to-all-start.1 = ((bf16[128,56,128]{2,1,0:T(8,128)(2,1)}), bf16[128,56,128]{2,1,0:T(8,128)(2,1)S(1)}, u32[]{:S(2)}, u32[]{:S(2)}) async-start(bf16[128,56,128]{2,1,0:T(8,128)(2,1)} %reshape.129), calls=%async_computation.1 | async-start | bytes 3670016 | tf_op jit(solution)/shard_map/all_to_all | solution.py:88
  145.0 24.3 %slice-start = ((s8[7340032]{0:T(1024)(128)(4,1)}), s8[4194304]{0:T(1024)(128)(4,1)S(1)}, s32[]{:S(2)}) async-start(s8[7340032]{0:T(1024)(128)(4,1)} %bitcast.67), calls=%async_computation.4 | async-start | bytes 8388608
  156.3 12.9 %slice-start.1 = ((s8[7340032]{0:T(1024)(128)(4,1)}), s8[3145728]{0:T(1024)(128)(4,1)S(1)}, s32[]{:S(2)}) async-start(s8[7340032]{0:T(1024)(128)(4,1)} %bitcast.67), calls=%async_computation.5 | async-start | bytes 6291456
  179.1 97.9 %all-to-all-start.3 = ((bf16[128,8,3584]{2,1,0:T(8,128)(2,1)}), bf16[128,8,3584]{2,1,0:T(8,128)(2,1)}, u32[]{:S(2)}, u32[]{:S(2)}) async-start(bf16[128,8,3584]{2,1,0:T(8,128)(2,1)} %fusion.16), calls=%async_computation.3 | async-start | bytes 14680064 | tf_op jit(solution)/shard_map/all_to_all | solution.py:88
  277.1 5.3 %copy-start.1 = (f32[256,3584]{1,0:T(8,128)S(1)}, f32[256,3584]{1,0:T(8,128)}, u32[]{:S(2)}) copy-start(f32[256,3584]{1,0:T(8,128)} %fusion.54) | copy-start | bytes 11010052
